TPU v7x, 128 devices: a whole 4x4x4 slice. The times are simulated.
128 devices in a mesh: lon: 16 (over y, z_hi, core), lat: 8 (over x, z_lo).
Axes of the slice: x: 4, y: 4, z: 4 (z_hi: 2, z_lo: 2; z = z_hi * 2 + z_lo), core: 2. Of those that a mesh axis runs over, the one named last changes fastest.
Arguments:
- innovations: float32 [150, 65536], P(None, ('lon', 'lat')), may hold values from -6 to 6
- owner_tile: int32 [65536, 1], P(('lon', 'lat')), may hold values from 0 to 127; in each aligned block of 512 rows (0 to 511, 512 to 1023, ...) at most 16 rows name the same one
- obs_column: int32 [65536], P(('lon', 'lat')), may hold values from 0 to 8191
- obs_depth: int32 [65536], P(('lon', 'lat')), may hold values from 1 to 75
- coefficients: float32 [9, 512, 2048], P(None, 'lat', 'lon'), may hold values from 0.03 to 0.25
- sea_depth: int32 [512, 2048], P('lat', 'lon'), may hold values from 0 to 75
- balance: float32 [150, 150], replicated, may hold values from -0.5 to 0.5
Outputs:
- gradient: float32 [150, 512, 2048], P(None, 'lat', 'lon')
Inputs may be any that keep to these rules, and one draw needn't show every extreme that they name: `owner_tile`: among the 512 profiles of one device, at most 16 share one owner tile, and some device holds exactly 16 for one owner.
All inputs are finite; a program needn't handle non-finite values.
Results may differ from a plain program's by a relative error of at most 0.00012.
Values sent between devices are 32-bit elements; how exact they have to be, the bound alone decides.
No kernel may reach another device: no remote copies, remote signals or barrier semaphores. Data moves between devices by JAX's collectives and lax.ppermute only.
A program may use at most 128 MiB of HBM per device.

v0:
```python
import jax
import jax.numpy as jnp
from jax import lax
from jax.sharding import PartitionSpec as P

LEVELS = 75
PASSES = 4


def padded_2(block, sides, width, periodic):
    for axis, dim in sides:
        count = lax.axis_size(axis)
        forward = [(i, i + 1) for i in range(count - 1)]
        if periodic:
            forward.append((count - 1, 0))
        backward = [(target, source) for source, target in forward]
        low = lax.ppermute(
            lax.slice_in_dim(block, block.shape[dim] - width, None, axis=dim), axis, forward
        )
        high = lax.ppermute(lax.slice_in_dim(block, 0, width, axis=dim), axis, backward)
        block = jnp.concatenate([low, block, high], axis=dim)
    return block


def adjoint_stencil(padded, coef_pad):
    extent_y = padded.shape[1] - 2
    extent_x = padded.shape[2] - 2
    summed = jnp.zeros((padded.shape[0], extent_y, extent_x), jnp.float32)
    for step_y in (-1, 0, 1):
        for step_x in (-1, 0, 1):
            offset = (step_y + 1) * 3 + step_x + 1
            row_start = 1 - step_y
            col_start = 1 - step_x
            summed = (
                summed
                + coef_pad[
                    offset, row_start : row_start + extent_y, col_start : col_start + extent_x
                ][None]
                * padded[:, row_start : row_start + extent_y, col_start : col_start + extent_x]
            )
    return summed


def mix_levels(field, balance):
    return jnp.einsum("cyx,cd->dyx", field, balance, precision=lax.Precision.HIGHEST)


def local(innovations, owner_tile, obs_column, obs_depth, coefficients, sea_depth, balance):
    channels = innovations.shape[0]
    obs_count = innovations.shape[1]
    lon_count = lax.axis_size("lon")
    lat_count = lax.axis_size("lat")
    devices = lon_count * lat_count
    capacity = 4 * obs_count // devices
    level_ids = jnp.arange(channels) % LEVELS
    level_float = level_ids.astype(jnp.float32)
    kept = jnp.where(level_ids[:, None] < obs_depth[None, :], innovations, 0.0)
    targets = owner_tile[:, 0]
    one_hot = (targets[:, None] == jnp.arange(devices, dtype=jnp.int32)[None, :]).astype(jnp.int32)
    before = jnp.cumsum(one_hot, axis=0) - one_hot
    slot_rank = jnp.sum(before * one_hot, axis=1)
    destination = targets * capacity + slot_rank
    send_values = (
        jnp.zeros((channels, devices * capacity), jnp.float32).at[:, destination].set(kept)
    )
    send_columns = jnp.zeros((1, devices * capacity), jnp.int32).at[0, destination].set(obs_column)
    got_values, got_columns = (
        lax.all_to_all(send_values, ("lon", "lat"), split_axis=1, concat_axis=1, tiled=True),
        lax.all_to_all(send_columns, ("lon", "lat"), split_axis=1, concat_axis=1, tiled=True),
    )
    rows_y = sea_depth.shape[0]
    cols_x = sea_depth.shape[1]
    field = (
        jnp.zeros((channels, rows_y * cols_x), jnp.float32).at[:, got_columns[0]].add(got_values)
    )
    field = field.reshape(channels, rows_y, cols_x)
    depth_float = sea_depth.astype(jnp.float32)
    stacked = jnp.concatenate([coefficients, depth_float[None]], axis=0)
    stacked = padded_2(stacked, (("lat", 1),), PASSES, False)
    stacked = padded_2(stacked, (("lon", 2),), PASSES, True)
    padded = padded_2(field, (("lat", 1),), PASSES, False)
    padded = padded_2(padded, (("lon", 2),), PASSES, True)
    for pass_index in range(PASSES):
        radius = PASSES - pass_index
        span_y = rows_y + 2 * radius
        span_x = cols_x + 2 * radius
        coef_view = stacked[:9, pass_index : pass_index + span_y, pass_index : pass_index + span_x]
        depth_view = stacked[
            9, pass_index + 1 : pass_index + span_y - 1, pass_index + 1 : pass_index + span_x - 1
        ]
        wet_view = (level_float[:, None, None] < depth_view[None]).astype(jnp.float32)
        padded = mix_levels(wet_view * adjoint_stencil(padded, coef_view), balance)
    field = padded
    return field


def solution(mesh):
    placed = (
        P(None, ("lon", "lat")),
        P(("lon", "lat"), None),
        P(("lon", "lat")),
        P(("lon", "lat")),
        P(None, "lat", "lon"),
        P("lat", "lon"),
        P(),
    )
    return jax.shard_map(
        local, mesh=mesh, in_specs=placed, out_specs=P(None, "lat", "lon"), check_vma=False
    )
```

profile of v0, /device:TPU:34, one launch (start us, length us, event | category | flops | bytes accessed | tf_op | source)
XLA Modules:
  0.0 284.5 jit_solution(2208196743894323249)
XLA Ops:
  0.0 0.8 copy.19
  0.8 0.2 fusion.142
  1.2 0.9 fusion.141
  2.1 0.7 compare_select_fusion.1
  2.8 2.6 scatter_custom_fusion
  5.4 0.7 all_to_all.14
  6.1 10.2 %all-to-all-start = ((s32[1,128,16]{2,0,1:T(1,128)}), s32[1,128,16]{2,0,1:T(1,128)S(1)}, u32[]{:S(2)}, u32[]{:S(2)}) async-start(s32[1,128,16]{2,0,1:T(1,128)} %bitcast.15), calls=%async_computation | async-start | bytes 131072 | tf_op jit(solution)/shard_map/all_to_all | solution.py:69
  16.3 0.8 fusion.162
  17.1 0.8 pad_maximum_fusion.19
  17.9 2.3 collective-permute-start.1
  20.2 4.4 %collective-permute-start = (f32[10,4,128]{2,1,0:T(4,128)S(1)}, f32[10,4,128]{2,1,0:T(4,128)S(1)}, u32[]{:S(2)}, u32[]{:S(2)}) collective-permute-start(f32[10,4,128]{2,1,0:T(4,128)S(1)} %get-tuple-element.49), channel_id=1, source_target_pairs={{0,1},{1,2},{2,3},{3,4},{4,5},{5,6},{6,7},{8,9},{9,10},{10,11},{11... | collective-permute-start | bytes 61448 | tf_op jit(solution)/shard_map/ppermute | solution.py:17
  24.6 1.1 select_bitcast_fusion
  25.7 0.2 copy.22
  25.9 3.6 %scatter_custom_fusion.1 = f32[150,2048]{0,1:T(8,128)} fusion(s32[512]{0:T(512)S(1)} %bitcast.146, f32[512,150]{1,0:T(8,128)S(1)} %copy.22, f32[]{:T(128)} %constant.18.clone.1), kind=kCustom, calls=%fused_computation.138 | custom fusion | bytes 1228804 | tf_op jit(solution)/shard_map/scatter | solution.py:64
  29.6 10.2 %all-to-all-start.1 = ((f32[150,128,16]{0,2,1:T(8,128)}), f32[150,128,16]{0,2,1:T(8,128)}, u32[]{:S(2)}, u32[]{:S(2)}) async-start(f32[150,128,16]{0,2,1:T(8,128)} %bitcast.18), calls=%async_computation.1 | async-start | bytes 4194304 | tf_op jit(solution)/shard_map/all_to_all | solution.py:68
  39.8 0.6 broadcast.136
  40.3 0.8 reduce.3
  41.1 0.1 squeeze.4
  41.2 0.0 collective-permute-done
  41.3 0.2 fusion.161
  41.5 4.7 %collective-permute-start.2 = (f32[10,72,4]{2,1,0:T(8,128)S(1)}, f32[10,72,4]{2,1,0:T(8,128)S(1)}, u32[]{:S(2)}, u32[]{:S(2)}) collective-permute-start(f32[10,72,4]{2,1,0:T(8,128)S(1)} %get-tuple-element.46), channel_id=1, source_target_pairs={{8,0},{16,8},{24,16},{32,24},{40,32},{48,40},{56,48},{64,56},{72,6... | collective-permute-start | bytes 34568 | tf_op jit(solution)/shard_map/ppermute | solution.py:20
  46.2 0.0 collective-permute-start.3
  46.2 19.7 %collective-permute-done.2 = f32[10,72,4]{2,1,0:T(8,128)S(1)} collective-permute-done((f32[10,72,4]{2,1,0:T(8,128)S(1)}, f32[10,72,4]{2,1,0:T(8,128)S(1)}, u32[]{:S(2)}, u32[]{:S(2)}) %collective-permute-start.2) | collective-permute-done | bytes 11552 | tf_op jit(solution)/shard_map/ppermute | solution.py:20
  65.9 5.0 %collective-permute-done.3 = f32[10,72,4]{2,1,0:T(8,128)S(1)} collective-permute-done((f32[10,72,4]{2,1,0:T(8,128)S(1)}, f32[10,72,4]{2,1,0:T(8,128)S(1)}, u32[]{:S(2)}, u32[]{:S(2)}) %collective-permute-start.3) | collective-permute-done | bytes 11552 | tf_op jit(solution)/shard_map/ppermute | solution.py:17
  70.9 0.4 pad_maximum_fusion.1
  71.4 0.1 maximum_bitcast_fusion.9
  71.5 0.1 slice_bitcast_fusion.23
  71.6 0.2 slice_bitcast_fusion.20
  71.9 17.0 %scatter_custom_fusion.2 = f32[150,8192]{0,1:T(8,128)} fusion(s32[2048]{0:T(1024)S(1)} %bitcast.144, f32[2048,150]{1,0:T(8,128)} %bitcast.20, f32[]{:T(128)} %constant.18.clone.1), kind=kCustom, calls=%fused_computation.129 | custom fusion | flops 307200 | bytes 4915712 | tf_op jit(solution)/shard_map/scatter-add | solution.py:74
  88.8 1.4 fusion.160
  90.3 2.8 collective-permute-start.5
  93.1 4.0 %collective-permute-start.4 = (f32[150,4,128]{0,2,1:T(8,128)S(1)}, f32[150,4,128]{0,2,1:T(8,128)S(1)}, u32[]{:S(2)}, u32[]{:S(2)}) collective-permute-start(f32[150,4,128]{0,2,1:T(8,128)S(1)} %get-tuple-element.7), channel_id=1, source_target_pairs={{0,1},{1,2},{2,3},{3,4},{4,5},{5,6},{6,7},{8,9},{9,10},{10,11},{11... | collective-permute-start | bytes 921608 | tf_op jit(solution)/shard_map/ppermute | solution.py:17
  97.1 0.2 maximum_bitcast_fusion.4
  97.3 0.3 slice_bitcast_fusion.22
  97.6 16.7 %collective-permute-done.5 = f32[150,4,128]{0,2,1:T(8,128)S(1)} collective-permute-done((f32[150,4,128]{0,2,1:T(8,128)S(1)}, f32[150,4,128]{0,2,1:T(8,128)S(1)}, u32[]{:S(2)}, u32[]{:S(2)}) %collective-permute-start.5) | collective-permute-done | bytes 307232 | tf_op jit(solution)/shard_map/ppermute | solution.py:20
  114.3 4.8 %collective-permute-done.4 = f32[150,4,128]{0,2,1:T(8,128)S(1)} collective-permute-done((f32[150,4,128]{0,2,1:T(8,128)S(1)}, f32[150,4,128]{0,2,1:T(8,128)S(1)}, u32[]{:S(2)}, u32[]{:S(2)}) %collective-permute-start.4) | collective-permute-done | bytes 307232 | tf_op jit(solution)/shard_map/ppermute | solution.py:17
  119.1 1.3 pad_maximum_fusion.5
  120.4 0.3 collective-permute-start.7
  120.7 0.5 collective-permute-start.6
  121.2 0.1 maximum_bitcast_fusion.8
  121.4 3.6 %collective-permute-done.7 = f32[150,72,4]{0,2,1:T(4,128)S(1)} collective-permute-done((f32[150,72,4]{0,2,1:T(4,128)S(1)}, f32[150,72,4]{0,2,1:T(4,128)S(1)}, u32[]{:S(2)}, u32[]{:S(2)}) %collective-permute-start.7) | collective-permute-done | bytes 172832 | tf_op jit(solution)/shard_map/ppermute | solution.py:20
  124.9 5.7 %collective-permute-done.6 = f32[150,72,4]{0,2,1:T(4,128)S(1)} collective-permute-done((f32[150,72,4]{0,2,1:T(4,128)S(1)}, f32[150,72,4]{0,2,1:T(4,128)S(1)}, u32[]{:S(2)}, u32[]{:S(2)}) %collective-permute-start.6) | collective-permute-done | bytes 172832 | tf_op jit(solution)/shard_map/ppermute | solution.py:17
  130.6 4.6 %pad_maximum_fusion = f32[150,72,136]{0,2,1:T(8,128)S(1)} fusion(f32[150,72,4]{0,2,1:T(4,128)S(1)} %collective-permute-done.7, f32[150,4,128]{0,2,1:T(8,128)S(1)} %collective-permute-done.5, f32[150,64,128]{0,2,1:T(8,128)S(1)} %bitcast.137, f32[150,4,128]{0,2,1:T(8,128)S(1)} %collective-permute-done.4, f32[150,72,4]{0,2,1:T(4,128)S(1)} %collective-permute-done.6), kind=kLoop, calls=%fused_computation.3 | loop fusion | flops 5875200 | bytes 11750400 | tf_op jit(solution)/shard_map/concatenate | solution.py:21
  135.3 35.2 %fusion.126 = f32[150,70,134]{0,2,1:T(8,128)S(1)} fusion(f32[150,72,136]{0,2,1:T(8,128)S(1)} %pad_maximum_fusion, f32[70,134]{1,0:T(8,128)S(1)} %get-tuple-element.36, f32[70,134]{1,0:T(8,128)S(1)} %get-tuple-element.37, f32[70,134]{1,0:T(8,128)S(1)} %get-tuple-element.38, f32[70,134]{1,0:T(8,128)S(1)} %get-tuple-element.39, ...), kind=kOutput, calls=%fused_computation.134 | convolution fusion | flops 2559333120 | bytes 94258272 | tf_op jit(solution)/shard_map/cyx,cd->dyx/dot_general | solution.py:45
  170.5 34.1 %fusion.129 = f32[150,68,132]{0,2,1:T(8,128)S(1)} fusion(f32[150,70,134]{0,2,1:T(8,128)S(1)} %fusion.126, f32[68,132]{1,0:T(8,128)S(1)} %get-tuple-element.26, f32[68,132]{1,0:T(8,128)S(1)} %get-tuple-element.27, f32[68,132]{1,0:T(8,128)S(1)} %get-tuple-element.28, f32[68,132]{1,0:T(8,128)S(1)} %get-tuple-element.29, f32[68,132]{1,0:T(8,128)S(1)} %get-tuple-element.30, ...), kind=kOutput, calls=%fused_computation.135 | convolution fusion | flops 2449101568 | bytes 91509120 | tf_op jit(solution)/shard_map/cyx,cd->dyx/dot_general | solution.py:45
  204.6 32.9 %fusion.132 = f32[150,66,130]{0,2,1:T(8,128)S(1)} fusion(f32[150,68,132]{0,2,1:T(8,128)S(1)} %fusion.129, f32[66,130]{1,0:T(8,128)S(1)} %get-tuple-element.23, f32[66,130]{1,0:T(8,128)S(1)} %get-tuple-element.16, f32[66,130]{1,0:T(8,128)S(1)} %get-tuple-element.20, f32[66,130]{1,0:T(8,128)S(1)} %get-tuple-element.24, f32[66,130]{1,0:T(8,128)S(1)} %get-tuple-element.17, ...), kind=kOutput, calls=%fused_computation.136 | convolution fusion | flops 2341053184 | bytes 88764768 | tf_op jit(solution)/shard_map/cyx,cd->dyx/dot_general | solution.py:45
  237.5 43.9 %fusion.135 = f32[150,64,128]{2,0,1:T(8,128)S(1)} fusion(f32[150,66,130]{0,2,1:T(8,128)S(1)} %fusion.132, f32[64,128]{1,0:T(8,128)S(1)} %get-tuple-element.14, f32[64,128]{1,0:T(8,128)S(1)} %get-tuple-element.47, f32[64,128]{1,0:T(8,128)S(1)} %get-tuple-element.11, f32[64,128]{1,0:T(8,128)S(1)} %get-tuple-element.13, f32[64,128]{1,0:T(8,128)S(1)} %get-tuple-element.51, ...), kind=kOutput, calls=%fused_computation.137 | convolution fusion | flops 2235187200 | bytes 80897024 | tf_op jit(solution)/shard_map/cyx,cd->dyx/dot_general | solution.py:45
  281.4 3.1 %copy.25 = f32[150,64,128]{2,1,0:T(8,128)} copy(f32[150,64,128]{2,0,1:T(8,128)S(1)} %fusion.135) | data formatting | bytes 9830400 | tf_op jit(solution)/shard_map/cyx,cd->dyx/dot_general | solution.py:45
  (23 shorter events, 0.2 us)
Async XLA Ops:
  0.0 135.3 %copy-start = (f32[150,150]{1,0:T(8,128)S(1)}, f32[150,150]{1,0:T(8,128)}, u32[]{:S(2)}) copy-start(f32[150,150]{1,0:T(8,128)} %param.13) | copy-start | bytes 270004
  0.0 41.2 %copy-start.1 = (f32[9,64,128]{2,1,0:T(8,128)S(1)}, f32[9,64,128]{2,1,0:T(8,128)}, u32[]{:S(2)}) copy-start(f32[9,64,128]{2,1,0:T(8,128)} %param.11) | copy-start | bytes 884740
  6.1 23.5 %all-to-all-start = ((s32[1,128,16]{2,0,1:T(1,128)}), s32[1,128,16]{2,0,1:T(1,128)S(1)}, u32[]{:S(2)}, u32[]{:S(2)}) async-start(s32[1,128,16]{2,0,1:T(1,128)} %bitcast.15), calls=%async_computation | async-start | bytes 131072 | tf_op jit(solution)/shard_map/all_to_all | solution.py:69
  17.9 23.4 %collective-permute-start.1 = (f32[10,4,128]{2,1,0:T(4,128)S(1)}, f32[10,4,128]{2,1,0:T(4,128)S(1)}, u32[]{:S(2)}, u32[]{:S(2)}) collective-permute-start(f32[10,4,128]{2,1,0:T(4,128)S(1)} %get-tuple-element.50), channel_id=1, source_target_pairs={{1,0},{2,1},{3,2},{4,3},{5,4},{6,5},{7,6},{9,8},{10,9},{11,10},{12... | collective-permute-start | bytes 61448 | tf_op jit(solution)/shard_map/ppermute | solution.py:20
  20.2 21.0 %collective-permute-start = (f32[10,4,128]{2,1,0:T(4,128)S(1)}, f32[10,4,128]{2,1,0:T(4,128)S(1)}, u32[]{:S(2)}, u32[]{:S(2)}) collective-permute-start(f32[10,4,128]{2,1,0:T(4,128)S(1)} %get-tuple-element.49), channel_id=1, source_target_pairs={{0,1},{1,2},{2,3},{3,4},{4,5},{5,6},{6,7},{8,9},{9,10},{10,11},{11... | collective-permute-start | bytes 61448 | tf_op jit(solution)/shard_map/ppermute | solution.py:17
  29.6 42.3 %all-to-all-start.1 = ((f32[150,128,16]{0,2,1:T(8,128)}), f32[150,128,16]{0,2,1:T(8,128)}, u32[]{:S(2)}, u32[]{:S(2)}) async-start(f32[150,128,16]{0,2,1:T(8,128)} %bitcast.18), calls=%async_computation.1 | async-start | bytes 4194304 | tf_op jit(solution)/shard_map/all_to_all | solution.py:68
  41.5 24.4 %collective-permute-start.2 = (f32[10,72,4]{2,1,0:T(8,128)S(1)}, f32[10,72,4]{2,1,0:T(8,128)S(1)}, u32[]{:S(2)}, u32[]{:S(2)}) collective-permute-start(f32[10,72,4]{2,1,0:T(8,128)S(1)} %get-tuple-element.46), channel_id=1, source_target_pairs={{8,0},{16,8},{24,16},{32,24},{40,32},{48,40},{56,48},{64,56},{72,6... | collective-permute-start | bytes 34568 | tf_op jit(solution)/shard_map/ppermute | solution.py:20
  46.2 24.8 %collective-permute-start.3 = (f32[10,72,4]{2,1,0:T(8,128)S(1)}, f32[10,72,4]{2,1,0:T(8,128)S(1)}, u32[]{:S(2)}, u32[]{:S(2)}) collective-permute-start(f32[10,72,4]{2,1,0:T(8,128)S(1)} %get-tuple-element.45), channel_id=1, source_target_pairs={{0,8},{8,16},{16,24},{24,32},{32,40},{40,48},{48,56},{56,64},{64,7... | collective-permute-start | bytes 34568 | tf_op jit(solution)/shard_map/ppermute | solution.py:17
  88.8 41.8 %slice-start = ((s8[8388608]{0:T(1024)(128)(4,1)}), s8[4194304]{0:T(1024)(128)(4,1)S(1)}, s32[]{:S(2)}) async-start(s8[8388608]{0:T(1024)(128)(4,1)} %bitcast.135), calls=%async_computation.2 | async-start | bytes 8388608
  90.3 24.1 %collective-permute-start.5 = (f32[150,4,128]{0,2,1:T(8,128)S(1)}, f32[150,4,128]{0,2,1:T(8,128)S(1)}, u32[]{:S(2)}, u32[]{:S(2)}) collective-permute-start(f32[150,4,128]{0,2,1:T(8,128)S(1)} %get-tuple-element.8), channel_id=1, source_target_pairs={{1,0},{2,1},{3,2},{4,3},{5,4},{6,5},{7,6},{9,8},{10,9},{11,10},{12... | collective-permute-start | bytes 921608 | tf_op jit(solution)/shard_map/ppermute | solution.py:20
  93.1 26.0 %collective-permute-start.4 = (f32[150,4,128]{0,2,1:T(8,128)S(1)}, f32[150,4,128]{0,2,1:T(8,128)S(1)}, u32[]{:S(2)}, u32[]{:S(2)}) collective-permute-start(f32[150,4,128]{0,2,1:T(8,128)S(1)} %get-tuple-element.7), channel_id=1, source_target_pairs={{0,1},{1,2},{2,3},{3,4},{4,5},{5,6},{6,7},{8,9},{9,10},{10,11},{11... | collective-permute-start | bytes 921608 | tf_op jit(solution)/shard_map/ppermute | solution.py:17
  97.6 33.0 %slice-start.1 = ((s8[8388608]{0:T(1024)(128)(4,1)}), s8[4194304]{0:T(1024)(128)(4,1)S(1)}, s32[]{:S(2)}) async-start(s8[8388608]{0:T(1024)(128)(4,1)} %bitcast.135), calls=%async_computation.3 | async-start | bytes 8388608
  120.4 4.5 %collective-permute-start.7 = (f32[150,72,4]{0,2,1:T(4,128)S(1)}, f32[150,72,4]{0,2,1:T(4,128)S(1)}, u32[]{:S(2)}, u32[]{:S(2)}) collective-permute-start(f32[150,72,4]{0,2,1:T(4,128)S(1)} %get-tuple-element.6), channel_id=1, source_target_pairs={{8,0},{16,8},{24,16},{32,24},{40,32},{48,40},{56,48},{64,56},{72,6... | collective-permute-start | bytes 518408 | tf_op jit(solution)/shard_map/ppermute | solution.py:20
  120.7 9.9 %collective-permute-start.6 = (f32[150,72,4]{0,2,1:T(4,128)S(1)}, f32[150,72,4]{0,2,1:T(4,128)S(1)}, u32[]{:S(2)}, u32[]{:S(2)}) collective-permute-start(f32[150,72,4]{0,2,1:T(4,128)S(1)} %get-tuple-element.5), channel_id=1, source_target_pairs={{0,8},{8,16},{16,24},{24,32},{32,40},{40,48},{48,56},{56,64},{64,7... | collective-permute-start | bytes 518408 | tf_op jit(solution)/shard_map/ppermute | solution.py:17
where the time goes:
time: 287 us; the launch traced here: 285 us
  matrix products  146 us (51%)
  waiting for transfers between devices  55.5 us (19%)
  starting transfers between devices  39.5 us (14%)
  other arithmetic  29.1 us (10%)
  local copies, waits for them, and re-layouts  14 us (5%)
    dot_general x4, matrix products, mix_levels(): jnp.einsum('cyx,cd->dyx', field, balance, precision=lax.Precision.HIGHEST)  146 us
    ppermute x4, waiting for transfers between devices, padded_2(): lax.ppermute(lax.slice_in_dim(block, 0, width, axis=dim), axis, backward)  40 us
    scatter-add x1, other arithmetic, local(): jnp.zeros((channels, rows_y * cols_x), jnp.float32).at[:, got_columns[0]]  17 us
    ppermute x4, waiting for transfers between devices, padded_2(): lax.ppermute(lax.slice_in_dim(block, block.shape[dim] - width, None, axis...  15.5 us
    all_to_all x1, starting transfers between devices, local(): lax.all_to_all(send_columns, ('lon', 'lat'), split_axis=1, concat_axis=1,...  10.2 us
    all_to_all x1, starting transfers between devices, local(): lax.all_to_all(send_values, ('lon', 'lat'), split_axis=1, concat_axis=1,...  10.2 us
    ppermute x4, starting transfers between devices, padded_2(): lax.ppermute(lax.slice_in_dim(block, 0, width, axis=dim), axis, backward)  10.1 us
    ppermute x4, starting transfers between devices, padded_2(): lax.ppermute(lax.slice_in_dim(block, block.shape[dim] - width, None, axis...  8.95 us
  transfers between devices with their start and end apart: 10, of which 6 were waited for; matrix products, arithmetic and copies ran while one was open for 3% of the time, Pallas kernels for 0%

commit v1 on v0

v1 whole, which is shorter than its diff:
```python
import jax
import jax.numpy as jnp
from jax import lax
from jax.experimental import pallas as pl
from jax.experimental.pallas import tpu as pltpu
from jax.sharding import PartitionSpec as P

LEVELS = 75
PASSES = 4
RADIUS = PASSES
LANES = 256
CPAD = 152
CHUNK = 8


def shift_lon(block, step):
    count = lax.axis_size("lon")
    return lax.ppermute(block, "lon", [(i, (i + step) % count) for i in range(count)])


def shift_lat(block, step):
    count = lax.axis_size("lat")
    return lax.ppermute(
        block, "lat", [(i, i + step) for i in range(count) if 0 <= i + step < count]
    )


def shift_both(block, step_lon, step_lat):
    n_lon = lax.axis_size("lon")
    n_lat = lax.axis_size("lat")
    pairs = []
    for i in range(n_lon):
        for j in range(n_lat):
            if 0 <= j + step_lat < n_lat:
                pairs.append((i * n_lat + j, ((i + step_lon) % n_lon) * n_lat + j + step_lat))
    return lax.ppermute(block, ("lon", "lat"), pairs)


def with_halo(v):
    rows, ch, cols = v.shape
    r = RADIUS

    def dense(a):
        return a.reshape(a.shape[0], ch * r)

    def back(a, n):
        return a.reshape(n, ch, r)

    west = back(shift_lon(dense(v[:, :, cols - r :]), 1), rows)
    east = back(shift_lon(dense(v[:, :, :r]), -1), rows)
    south = shift_lat(v[rows - r :], 1)
    north = shift_lat(v[:r], -1)
    sw = back(shift_both(dense(v[rows - r :, :, cols - r :]), 1, 1), r)
    se = back(shift_both(dense(v[rows - r :, :, :r]), -1, 1), r)
    nw = back(shift_both(dense(v[:r, :, cols - r :]), 1, -1), r)
    ne = back(shift_both(dense(v[:r, :, :r]), -1, -1), r)
    top = jnp.concatenate([sw, south, se], axis=2)
    mid = jnp.concatenate([west, v, east], axis=2)
    bot = jnp.concatenate([nw, north, ne], axis=2)
    full = jnp.concatenate([top, mid, bot], axis=0)
    return jnp.pad(full, ((0, 0), (0, 0), (0, LANES - cols - 2 * r)))


def passes_kernel(p_ref, s_ref, lvl_ref, bal_ref, out_ref, a_ref, b_ref, u_ref):
    full = p_ref.shape[0]
    chans = p_ref.shape[1]
    out_ch = out_ref.shape[1]
    out_x = out_ref.shape[2]
    srcs = [p_ref, a_ref, b_ref, a_ref]
    dsts = [a_ref, b_ref, a_ref, None]
    for p in range(PASSES):
        src = srcs[p]
        dst = dsts[p]

        def row(y, carry, src=src, dst=dst):
            srows = [s_ref[y - dy] for dy in (-1, 0, 1)]
            coefs = {}
            for dy in (-1, 0, 1):
                for dx in (-1, 0, 1):
                    k = (dy + 1) * 3 + dx + 1
                    coefs[(dy, dx)] = jnp.broadcast_to(
                        srows[dy + 1][k : k + 1, :], (CHUNK, LANES)
                    )
            depth = jnp.broadcast_to(srows[1][9:10, :], (CHUNK, LANES))
            for c0 in range(0, chans, CHUNK):
                sums = [None, None, None]
                for dy in (-1, 0, 1):
                    v = src[y - dy, c0 : c0 + CHUNK, :]
                    for dx in (-1, 0, 1):
                        t = coefs[(dy, dx)] * v
                        sums[dx + 1] = t if sums[dx + 1] is None else sums[dx + 1] + t
                acc = (
                    sums[1]
                    + pltpu.roll(sums[0], LANES - 1, 1)
                    + pltpu.roll(sums[2], 1, 1)
                )
                u_ref[c0 : c0 + CHUNK, :] = jnp.where(
                    lvl_ref[c0 : c0 + CHUNK, :] < depth, acc, 0.0
                )
            res = jnp.dot(
                bal_ref[...],
                u_ref[...],
                precision=lax.Precision.HIGHEST,
                preferred_element_type=jnp.float32,
            )
            if dst is None:
                shifted = pltpu.roll(res, LANES - RADIUS, 1)
                out_ref[y - RADIUS] = shifted[:out_ch, :out_x]
            else:
                dst[y] = res
            return carry

        lax.fori_loop(p + 1, full - 1 - p, row, 0)


def run_passes(padded, stat, balance, rows, chans, cols):
    full = padded.shape[0]
    lvl = jnp.broadcast_to(
        (jnp.arange(CPAD) % LEVELS).astype(jnp.float32)[:, None], (CPAD, LANES)
    )
    bal_t = jnp.pad(balance.T, ((0, CPAD - chans), (0, CPAD - chans)))
    vmem = pltpu.VMEM
    work = full * CPAD * LANES
    return pl.pallas_call(
        passes_kernel,
        out_shape=jax.ShapeDtypeStruct((rows, chans, cols), jnp.float32),
        in_specs=[pl.BlockSpec(memory_space=vmem)] * 4,
        out_specs=pl.BlockSpec(memory_space=vmem),
        scratch_shapes=[
            vmem(padded.shape, jnp.float32),
            vmem(padded.shape, jnp.float32),
            vmem((CPAD, LANES), jnp.float32),
        ],
        compiler_params=pltpu.CompilerParams(vmem_limit_bytes=62 * 1024 * 1024),
        cost_estimate=pl.CostEstimate(
            flops=PASSES * (work * 20 + 2 * full * CPAD * CPAD * LANES),
            bytes_accessed=4 * (work + rows * chans * cols),
            transcendentals=0,
        ),
    )(padded, stat, lvl, bal_t)


def local(innovations, owner_tile, obs_column, obs_depth, coefficients, sea_depth, balance):
    channels = innovations.shape[0]
    obs_count = innovations.shape[1]
    devices = lax.axis_size("lon") * lax.axis_size("lat")
    capacity = 4 * obs_count // devices
    rows_y = sea_depth.shape[0]
    cols_x = sea_depth.shape[1]

    stat = jnp.concatenate([coefficients, sea_depth.astype(jnp.float32)[None]], axis=0)
    stat = with_halo(jnp.transpose(stat, (1, 0, 2)))

    level_ids = jnp.arange(channels) % LEVELS
    kept = jnp.where(level_ids[:, None] < obs_depth[None, :], innovations, 0.0)
    targets = owner_tile[:, 0]
    one_hot = (targets[:, None] == jnp.arange(devices, dtype=jnp.int32)[None, :]).astype(jnp.int32)
    before = jnp.cumsum(one_hot, axis=0) - one_hot
    slot_rank = jnp.sum(before * one_hot, axis=1)
    destination = targets * capacity + slot_rank
    payload = jnp.concatenate([kept.T, obs_column.astype(jnp.float32)[:, None]], axis=1)
    send = jnp.zeros((devices * capacity, channels + 1), jnp.float32).at[destination].set(payload)
    got = lax.all_to_all(
        send.reshape(devices, capacity, channels + 1), ("lon", "lat"), 0, 0, tiled=True
    ).reshape(devices * capacity, channels + 1)
    where = got[:, channels].astype(jnp.int32)
    field = jnp.zeros((rows_y * cols_x, channels), jnp.float32).at[where].add(got[:, :channels])
    field = jnp.transpose(field.reshape(rows_y, cols_x, channels), (0, 2, 1))
    field = jnp.pad(field, ((0, 0), (0, CPAD - channels), (0, 0)))
    padded = with_halo(field)
    out = run_passes(padded, stat, balance, rows_y, channels, cols_x)
    return jnp.transpose(out, (1, 0, 2))


def solution(mesh):
    placed = (
        P(None, ("lon", "lat")),
        P(("lon", "lat"), None),
        P(("lon", "lat")),
        P(("lon", "lat")),
        P(None, "lat", "lon"),
        P("lat", "lon"),
        P(),
    )
    return jax.shard_map(
        local, mesh=mesh, in_specs=placed, out_specs=P(None, "lat", "lon"), check_vma=False
    )
```

time: 287 us -> 300 us (1.045)
  matrix products: 146 us -> 0 us
  Pallas kernels: 0 us -> 126 us
  waiting for transfers between devices: 55.5 us -> 2.27 us
  local copies, waits for them, and re-layouts: 14 us -> 61.5 us
  starting transfers between devices: 39.5 us -> 68.3 us
  other arithmetic: 29.1 us -> 39.7 us
    dot_general x4 -> x0, matrix products: 146 us -> none  [mix_levels(): jnp.einsum('cyx,cd->dyx', field, balance, precision=lax.Precision.HIGHEST)]
    pallas_call x0 -> x1, Pallas kernels: none -> 126 us  [run_passes(): pl.pallas_call(passes_kernel, out_shape=jax.ShapeDtypeStruct((rows, chans...]
    ppermute x8 -> x16, waiting for transfers between devices: 55.5 us -> 2.27 us  [the longest x8 2.24 us: shift_both(): return lax.ppermute(block, ('lon', 'lat'), pairs)]
    ppermute x8 -> x16, starting transfers between devices: 19.1 us -> 58.1 us  [the longest x8 34.4 us: shift_both(): return lax.ppermute(block, ('lon', 'lat'), pairs)]
    reshape x0 -> x21, local copies, waits for them, and re-layouts: none -> 20.9 us  [the longest x12 11.7 us: back(): return a.reshape(n, ch, r)]
    slice x2 -> x10, local copies, waits for them, and re-layouts: 1.59 us -> 22.5 us  [the longest x4 15.2 us: with_halo(): west = back(shift_lon(dense(v[:, :, cols - r:]), 1), rows)]
    concatenate x3, other arithmetic: 5.07 us -> 18 us  [the longest x2 17.9 us: with_halo(): full = jnp.concatenate([top, mid, bot], axis=0)]
    all_to_all x2 -> x1, starting transfers between devices: 20.4 us -> 10.2 us  [local(): lax.all_to_all(send.reshape(devices, capacity, channels + 1), ('lon', 'la...]
  transfers between devices with their start and end apart: 10 -> 17, of which waited for: 6 -> 1; matrix products, arithmetic and copies ran while one was open for 3% -> 23% of each run, Pallas kernels for 0% -> 0%
where the time goes in v1:
time: 300 us; the launch traced here: 298 us
  Pallas kernels  126 us (42%)
  starting transfers between devices  68.3 us (23%)
  local copies, waits for them, and re-layouts  61.5 us (20%)
  other arithmetic  39.7 us (13%)
    pallas_call x1, Pallas kernels, run_passes(): pl.pallas_call(passes_kernel, out_shape=jax.ShapeDtypeStruct((rows, chans...  126 us
    ppermute x8, starting transfers between devices, shift_both(): return lax.ppermute(block, ('lon', 'lat'), pairs)  34.4 us
    concatenate x2, other arithmetic, with_halo(): full = jnp.concatenate([top, mid, bot], axis=0)  17.9 us
    scatter-add x1, other arithmetic, local(): jnp.zeros((rows_y * cols_x, channels), jnp.float32).at[where]  16.8 us
    slice x4, local copies, waits for them, and re-layouts, with_halo(): west = back(shift_lon(dense(v[:, :, cols - r:]), 1), rows)  15.2 us
    ppermute x4, starting transfers between devices, shift_lat(): lax.ppermute(block, 'lat', [(i, i + step) for i in range(count) if 0 <= i...  12.8 us
    reshape x12, local copies, waits for them, and re-layouts, back(): return a.reshape(n, ch, r)  11.7 us
    ppermute x4, starting transfers between devices, shift_lon(): lax.ppermute(block, 'lon', [(i, (i + step) % count) for i in range(count)])  11 us
  transfers between devices with their start and end apart: 17, of which 1 were waited for; matrix products, arithmetic and copies ran while one was open for 23% of the time, Pallas kernels for 0%

profile of v1, /device:TPU:34, one launch (start us, length us, event | category | flops | bytes accessed | tf_op | source)
XLA Modules:
  0.0 297.9 jit_solution(1091921658862576448)
XLA Ops:
  0.0 0.8 copy.28
  0.8 0.2 fusion.12
  1.1 0.9 fusion.11
  2.0 0.7 compare_select_fusion.1
  2.7 0.7 convert_element_type.34
  3.4 1.1 select_bitcast_fusion
  4.7 3.6 %scatter_custom_fusion = f32[2048,151]{1,0:T(8,128)} fusion(s32[512]{0:T(512)S(1)} %bitcast.60, f32[512,151]{1,0:T(8,128)S(1)} %copy.30, f32[]{:T(128)} %constant.16.clone.1), kind=kCustom, calls=%fused_computation.26 | custom fusion | bytes 1236996 | tf_op jit(solution)/shard_map/scatter | solution.py:162
  8.4 10.2 %all-to-all-start = ((f32[128,16,151]{2,1,0:T(8,128)}), f32[128,16,151]{2,1,0:T(8,128)S(1)}, u32[]{:S(2)}, u32[]{:S(2)}) async-start(f32[128,16,151]{2,1,0:T(8,128)} %bitcast.45), calls=%async_computation | async-start | bytes 4194304 | tf_op jit(solution)/shard_map/all_to_all | solution.py:163
  19.1 3.0 collective-permute-start.8
  22.1 5.6 %collective-permute-start.10 = (f32[4,40]{1,0:T(4,128)S(1)}, f32[4,40]{1,0:T(4,128)S(1)}, u32[]{:S(2)}, u32[]{:S(2)}) collective-permute-start(f32[4,40]{1,0:T(4,128)S(1)} %reshape.136), channel_id=1, source_target_pairs={{0,121},{1,122},{2,123},{3,124},{4,125},{5,126},{6,127},{8,1},{9,2... | collective-permute-start | bytes 1928 | tf_op jit(solution)/shard_map/ppermute | solution.py:36
  27.8 1.9 collective-permute-start.13
  29.7 1.0 fusion.18
  30.8 1.2 copy.38
  32.0 0.8 copy.39
  32.8 5.5 %collective-permute-start.12 = (f32[64,40]{0,1:T(8,128)}, f32[64,40]{0,1:T(8,128)}, u32[]{:S(2)}, u32[]{:S(2)}) collective-permute-start(f32[64,40]{0,1:T(8,128)} %bitcast.21), channel_id=1, source_target_pairs={{0,120},{8,0},{16,8},{24,16},{32,24},{40,32},{48,40},{56,48},{64,5... | collective-permute-start | bytes 30728 | tf_op jit(solution)/shard_map/ppermute | solution.py:18
  38.3 0.6 fusion.15
  39.0 2.2 collective-permute-done.8
  41.2 7.3 %collective-permute-start.15 = (f32[4,40]{1,0:T(4,128)S(1)}, f32[4,40]{1,0:T(4,128)S(1)}, u32[]{:S(2)}, u32[]{:S(2)}) collective-permute-start(f32[4,40]{1,0:T(4,128)S(1)} %reshape.144), channel_id=1, source_target_pairs={{1,120},{2,121},{3,122},{4,123},{5,124},{6,125},{7,126},{9,0},{10,... | collective-permute-start | bytes 1928 | tf_op jit(solution)/shard_map/ppermute | solution.py:36
  48.6 0.7 pad.19.bal_ref
  49.4 2.2 collective-permute-start.14
  51.7 4.5 %collective-permute-start.9 = (f32[4,10,128]{2,1,0:T(8,128)S(1)}, f32[4,10,128]{2,1,0:T(8,128)S(1)}, u32[]{:S(2)}, u32[]{:S(2)}) collective-permute-start(f32[4,10,128]{2,1,0:T(8,128)S(1)} %get-tuple-element.17), channel_id=1, source_target_pairs={{0,1},{1,2},{2,3},{3,4},{4,5},{5,6},{6,7},{8,9},{9,10},{10,11},{11... | collective-permute-start | bytes 61448 | tf_op jit(solution)/shard_map/ppermute | solution.py:23
  56.4 0.7 reshape.145
  57.0 0.3 copy.40
  57.4 1.8 copy.41
  59.2 0.6 fusion.7
  59.8 16.8 %scatter_custom_fusion.1 = f32[8192,150]{1,0:T(8,128)} fusion(s32[2048]{0:T(1024)S(1)} %fusion.7, f32[]{:T(128)} %constant.16.clone.1, f32[2048,151]{1,0:T(8,128)S(1)} %bitcast.44), kind=kCustom, calls=%fused_computation.11 | custom fusion | flops 307200 | bytes 7012356 | tf_op jit(solution)/shard_map/scatter-add | solution.py:167
  76.6 8.3 %copy.32 = f32[64,128,150]{1,2,0:T(8,128)} copy(f32[64,128,150]{2,1,0:T(8,128)} %bitcast.41) | data formatting | bytes 9830400 | tf_op jit(solution)/shard_map/reshape | solution.py:168
  84.9 1.6 pad_slice_fusion.7
  86.5 1.2 copy-done
  87.6 0.9 pad_slice_fusion.6
  88.7 1.9 collective-permute-start
  90.8 6.2 %collective-permute-start.2 = (f32[4,608]{1,0:T(4,128)S(1)}, f32[4,608]{1,0:T(4,128)S(1)}, u32[]{:S(2)}, u32[]{:S(2)}) collective-permute-start(f32[4,608]{1,0:T(4,128)S(1)} %reshape.124), channel_id=1, source_target_pairs={{0,121},{1,122},{2,123},{3,124},{4,125},{5,126},{6,127},{8,1},{9,2... | collective-permute-start | bytes 29192 | tf_op jit(solution)/shard_map/ppermute | solution.py:36
  97.2 1.9 collective-permute-start.5
  99.1 3.6 %collective-permute-start.1 = (f32[4,152,128]{2,1,0:T(8,128)}, f32[4,152,128]{2,1,0:T(8,128)}, u32[]{:S(2)}, u32[]{:S(2)}) collective-permute-start(f32[4,152,128]{2,1,0:T(8,128)} %get-tuple-element.9), channel_id=1, source_target_pairs={{0,1},{1,2},{2,3},{3,4},{4,5},{5,6},{6,7},{8,9},{9,10},{10,11},{11... | collective-permute-start | bytes 933896 | tf_op jit(solution)/shard_map/ppermute | solution.py:23
  102.8 2.4 collective-permute-start.6
  105.2 9.0 %pad_slice_fusion.4 = (f32[64,152,4]{2,1,0:T(8,128)}, f32[64,152,4]{2,1,0:T(8,128)}) fusion(f32[64,150,128]{2,1,0:T(8,128)} %bitcast.38), kind=kLoop, calls=%fused_computation.49 | loop fusion | bytes 5226496 | tf_op jit(solution)/shard_map/slice | solution.py:49
  114.4 4.0 %copy.33 = f32[64,152,4]{0,2,1:T(4,128)S(1)} copy(f32[64,152,4]{2,1,0:T(8,128)} %get-tuple-element.11) | data formatting | bytes 311296 | tf_op jit(solution)/shard_map/slice | solution.py:49
  118.3 3.9 %copy.34 = f32[64,152,4]{0,2,1:T(4,128)S(1)} copy(f32[64,152,4]{2,1,0:T(8,128)} %get-tuple-element.12) | data formatting | bytes 311296 | tf_op jit(solution)/shard_map/slice | solution.py:50
  122.3 6.5 %collective-permute-start.7 = (f32[4,608]{1,0:T(4,128)S(1)}, f32[4,608]{1,0:T(4,128)S(1)}, u32[]{:S(2)}, u32[]{:S(2)}) collective-permute-start(f32[4,608]{1,0:T(4,128)S(1)} %reshape.132), channel_id=1, source_target_pairs={{1,120},{2,121},{3,122},{4,123},{5,124},{6,125},{7,126},{9,0},{10,... | collective-permute-start | bytes 29192 | tf_op jit(solution)/shard_map/ppermute | solution.py:36
  128.9 5.3 %collective-permute-start.4 = (f32[64,608]{0,1:T(8,128)S(1)}, f32[64,608]{0,1:T(8,128)}, u32[]{:S(2)}, u32[]{:S(2)}) collective-permute-start(f32[64,608]{0,1:T(8,128)S(1)} %bitcast.49), channel_id=1, source_target_pairs={{0,120},{8,0},{16,8},{24,16},{32,24},{40,32},{48,40},{56,48},{64,5... | collective-permute-start | bytes 466952 | tf_op jit(solution)/shard_map/ppermute | solution.py:18
  134.3 1.5 fusion.5.s_ref
  135.8 4.9 %pad.16 = f32[64,152,128]{2,1,0:T(8,128)} pad(f32[64,150,128]{2,1,0:T(8,128)} %bitcast.39, f32[]{:T(128)} %constant.16.clone.1), padding=0_0x0_2x0_0 | pad | bytes 9895940 | tf_op jit(solution)/shard_map/jit(_pad)/pad | solution.py:169
  141.4 3.7 %copy.35 = f32[64,152,4]{2,1,0:T(8,128)} copy(f32[64,152,4]{0,2,1:T(4,128)S(1)} %bitcast.51) | data formatting | bytes 311296 | tf_op jit(solution)/shard_map/reshape | solution.py:47
  145.1 4.4 %copy.36 = f32[64,152,4]{2,1,0:T(8,128)} copy(f32[64,152,4]{0,2,1:T(4,128)} %bitcast.16) | data formatting | bytes 311296 | tf_op jit(solution)/shard_map/reshape | solution.py:47
  149.4 16.4 %fusion.p_ref = f32[72,152,256]{2,1,0:T(8,128)} fusion(f32[4,152,4]{2,1,0:T(8,128)S(1)} %reshape.133, f32[4,152,128]{2,1,0:T(8,128)} %collective-permute-done.6, f32[4,152,4]{2,1,0:T(8,128)S(1)} %reshape.131, f32[64,152,4]{2,1,0:T(8,128)} %copy.36, f32[4,152,4]{2,1,0:T(8,128)S(1)} %reshape.125, f32[64,152,128]{2,1,0:T(8,128)} %pad.16, ...), kind=kLoop, calls=%fused_computation.3 | loop fusion | flops 50429952 | bytes 17160192 | tf_op jit(solution)/shard_map/concatenate | solution.py:60
  165.8 0.8 broadcast_in_dim.32.lvl_ref
  166.6 125.7 %shard_map.73 = f32[64,150,128]{2,1,0:T(8,128)} custom-call(f32[72,152,256]{2,1,0:T(8,128)} %fusion.p_ref, f32[72,10,256]{2,1,0:T(8,128)} %fusion.5.s_ref, f32[152,256]{1,0:T(8,128)} %broadcast_in_dim.32.lvl_ref, f32[152,152]{1,0:T(8,128)} %pad.19.bal_ref), custom_call_target="tpu_custom_call" | custom-call | flops 3630956544 | bytes 16121856 | tf_op jit(solution)/shard_map/pallas_call | solution.py:124
  292.3 5.6 %copy.43 = f32[150,64,128]{2,1,0:T(8,128)} copy(f32[150,64,128]{2,0,1:T(8,128)} %bitcast.42) | data formatting | bytes 9830400 | tf_op jit(solution)/shard_map/transpose | solution.py:172
  (69 shorter events, 2.8 us)
Async XLA Ops:
  0.8 17.8 %copy-start.2 = (f32[9,64,128]{2,1,0:T(8,128)S(1)}, f32[9,64,128]{2,1,0:T(8,128)}, u32[]{:S(2)}) copy-start(f32[9,64,128]{2,1,0:T(8,128)} %param.11) | copy-start | bytes 884740
  1.1 17.7 %copy-start.9 = (s32[64,128]{1,0:T(8,128)S(1)}, s32[64,128]{1,0:T(8,128)}, u32[]{:S(2)}) copy-start(s32[64,128]{1,0:T(8,128)} %param.12) | copy-start | bytes 98308
  8.4 40.2 %copy-start.3 = (f32[150,150]{1,0:T(8,128)S(1)}, f32[150,150]{1,0:T(8,128)}, u32[]{:S(2)}) copy-start(f32[150,150]{1,0:T(8,128)} %param.13) | copy-start | bytes 270004
  8.4 50.8 %all-to-all-start = ((f32[128,16,151]{2,1,0:T(8,128)}), f32[128,16,151]{2,1,0:T(8,128)S(1)}, u32[]{:S(2)}, u32[]{:S(2)}) async-start(f32[128,16,151]{2,1,0:T(8,128)} %bitcast.45), calls=%async_computation | async-start | bytes 4194304 | tf_op jit(solution)/shard_map/all_to_all | solution.py:163
  19.1 22.2 %collective-permute-start.8 = (f32[4,40]{1,0:T(4,128)S(1)}, f32[4,40]{1,0:T(4,128)S(1)}, u32[]{:S(2)}, u32[]{:S(2)}) collective-permute-start(f32[4,40]{1,0:T(4,128)S(1)} %reshape.134), channel_id=1, source_target_pairs={{0,9},{1,10},{2,11},{3,12},{4,13},{5,14},{6,15},{8,17},{9,18},{10,... | collective-permute-start | bytes 1928 | tf_op jit(solution)/shard_map/ppermute | solution.py:36
  22.1 27.3 %collective-permute-start.10 = (f32[4,40]{1,0:T(4,128)S(1)}, f32[4,40]{1,0:T(4,128)S(1)}, u32[]{:S(2)}, u32[]{:S(2)}) collective-permute-start(f32[4,40]{1,0:T(4,128)S(1)} %reshape.136), channel_id=1, source_target_pairs={{0,121},{1,122},{2,123},{3,124},{4,125},{5,126},{6,127},{8,1},{9,2... | collective-permute-start | bytes 1928 | tf_op jit(solution)/shard_map/ppermute | solution.py:36
  27.8 23.9 %collective-permute-start.13 = (f32[4,40]{1,0:T(4,128)S(1)}, f32[4,40]{1,0:T(4,128)S(1)}, u32[]{:S(2)}, u32[]{:S(2)}) collective-permute-start(f32[4,40]{1,0:T(4,128)S(1)} %reshape.142), channel_id=1, source_target_pairs={{1,8},{2,9},{3,10},{4,11},{5,12},{6,13},{7,14},{9,16},{10,17},{11,... | collective-permute-start | bytes 1928 | tf_op jit(solution)/shard_map/ppermute | solution.py:36
  32.0 25.1 %collective-permute-start.11 = (f32[64,40]{0,1:T(8,128)S(1)}, f32[64,40]{0,1:T(8,128)S(1)}, u32[]{:S(2)}, u32[]{:S(2)}) collective-permute-start(f32[64,40]{0,1:T(8,128)S(1)} %bitcast.53), channel_id=1, source_target_pairs={{0,8},{8,16},{16,24},{24,32},{32,40},{40,48},{48,56},{56,64},{64,7... | collective-permute-start | bytes 30728 | tf_op jit(solution)/shard_map/ppermute | solution.py:18
  32.8 24.5 %collective-permute-start.12 = (f32[64,40]{0,1:T(8,128)}, f32[64,40]{0,1:T(8,128)}, u32[]{:S(2)}, u32[]{:S(2)}) collective-permute-start(f32[64,40]{0,1:T(8,128)} %bitcast.21), channel_id=1, source_target_pairs={{0,120},{8,0},{16,8},{24,16},{32,24},{40,32},{48,40},{56,48},{64,5... | collective-permute-start | bytes 30728 | tf_op jit(solution)/shard_map/ppermute | solution.py:18
  41.2 15.1 %collective-permute-start.15 = (f32[4,40]{1,0:T(4,128)S(1)}, f32[4,40]{1,0:T(4,128)S(1)}, u32[]{:S(2)}, u32[]{:S(2)}) collective-permute-start(f32[4,40]{1,0:T(4,128)S(1)} %reshape.144), channel_id=1, source_target_pairs={{1,120},{2,121},{3,122},{4,123},{5,124},{6,125},{7,126},{9,0},{10,... | collective-permute-start | bytes 1928 | tf_op jit(solution)/shard_map/ppermute | solution.py:36
  49.4 49.7 %collective-permute-start.14 = (f32[4,10,128]{2,1,0:T(8,128)S(1)}, f32[4,10,128]{2,1,0:T(8,128)S(1)}, u32[]{:S(2)}, u32[]{:S(2)}) collective-permute-start(f32[4,10,128]{2,1,0:T(8,128)S(1)} %get-tuple-element.18), channel_id=1, source_target_pairs={{1,0},{2,1},{3,2},{4,3},{5,4},{6,5},{7,6},{9,8},{10,9},{11,10},{12... | collective-permute-start | bytes 61448 | tf_op jit(solution)/shard_map/ppermute | solution.py:23
  51.7 51.0 %collective-permute-start.9 = (f32[4,10,128]{2,1,0:T(8,128)S(1)}, f32[4,10,128]{2,1,0:T(8,128)S(1)}, u32[]{:S(2)}, u32[]{:S(2)}) collective-permute-start(f32[4,10,128]{2,1,0:T(8,128)S(1)} %get-tuple-element.17), channel_id=1, source_target_pairs={{0,1},{1,2},{2,3},{3,4},{4,5},{5,6},{6,7},{8,9},{9,10},{10,11},{11... | collective-permute-start | bytes 61448 | tf_op jit(solution)/shard_map/ppermute | solution.py:23
  84.9 2.8 copy-start
  88.7 33.6 %collective-permute-start = (f32[4,608]{1,0:T(4,128)S(1)}, f32[4,608]{1,0:T(4,128)S(1)}, u32[]{:S(2)}, u32[]{:S(2)}) collective-permute-start(f32[4,608]{1,0:T(4,128)S(1)} %reshape.122), channel_id=1, source_target_pairs={{0,9},{1,10},{2,11},{3,12},{4,13},{5,14},{6,15},{8,17},{9,18},{10,... | collective-permute-start | bytes 29192 | tf_op jit(solution)/shard_map/ppermute | solution.py:36
  90.8 38.0 %collective-permute-start.2 = (f32[4,608]{1,0:T(4,128)S(1)}, f32[4,608]{1,0:T(4,128)S(1)}, u32[]{:S(2)}, u32[]{:S(2)}) collective-permute-start(f32[4,608]{1,0:T(4,128)S(1)} %reshape.124), channel_id=1, source_target_pairs={{0,121},{1,122},{2,123},{3,124},{4,125},{5,126},{6,127},{8,1},{9,2... | collective-permute-start | bytes 29192 | tf_op jit(solution)/shard_map/ppermute | solution.py:36
  97.2 31.7 %collective-permute-start.5 = (f32[4,608]{1,0:T(4,128)S(1)}, f32[4,608]{1,0:T(4,128)S(1)}, u32[]{:S(2)}, u32[]{:S(2)}) collective-permute-start(f32[4,608]{1,0:T(4,128)S(1)} %reshape.130), channel_id=1, source_target_pairs={{1,8},{2,9},{3,10},{4,11},{5,12},{6,13},{7,14},{9,16},{10,17},{11,... | collective-permute-start | bytes 29192 | tf_op jit(solution)/shard_map/ppermute | solution.py:36
  99.1 15.1 %copy-start.5 = (f32[4,10,128]{2,1,0:T(8,128)}, f32[4,10,128]{2,1,0:T(8,128)S(1)}, u32[]{:S(2)}) copy-start(f32[4,10,128]{2,1,0:T(8,128)S(1)} %collective-permute-done.14) | copy-start | bytes 61444
  99.1 50.3 %collective-permute-start.1 = (f32[4,152,128]{2,1,0:T(8,128)}, f32[4,152,128]{2,1,0:T(8,128)}, u32[]{:S(2)}, u32[]{:S(2)}) collective-permute-start(f32[4,152,128]{2,1,0:T(8,128)} %get-tuple-element.9), channel_id=1, source_target_pairs={{0,1},{1,2},{2,3},{3,4},{4,5},{5,6},{6,7},{8,9},{9,10},{10,11},{11... | collective-permute-start | bytes 933896 | tf_op jit(solution)/shard_map/ppermute | solution.py:23
  102.8 11.4 %copy-start.7 = (f32[4,10,128]{2,1,0:T(8,128)}, f32[4,10,128]{2,1,0:T(8,128)S(1)}, u32[]{:S(2)}) copy-start(f32[4,10,128]{2,1,0:T(8,128)S(1)} %collective-permute-done.9) | copy-start | bytes 61444
  102.8 46.7 %collective-permute-start.6 = (f32[4,152,128]{2,1,0:T(8,128)}, f32[4,152,128]{2,1,0:T(8,128)}, u32[]{:S(2)}, u32[]{:S(2)}) collective-permute-start(f32[4,152,128]{2,1,0:T(8,128)} %get-tuple-element.10), channel_id=1, source_target_pairs={{1,0},{2,1},{3,2},{4,3},{5,4},{6,5},{7,6},{9,8},{10,9},{11,10},{12... | collective-permute-start | bytes 933896 | tf_op jit(solution)/shard_map/ppermute | solution.py:23
  114.3 19.9 %copy-start.1 = (f32[64,10,4]{2,1,0:T(8,128)S(1)}, f32[64,10,4]{2,1,0:T(8,128)}, u32[]{:S(2)}) copy-start(f32[64,10,4]{2,1,0:T(8,128)} %copy.41) | copy-start | bytes 30724
  114.4 19.9 %copy-start.4 = (f32[4,10,4]{2,1,0:T(8,128)S(1)}, f32[4,10,4]{2,1,0:T(8,128)}, u32[]{:S(2)}) copy-start(f32[4,10,4]{2,1,0:T(8,128)} %reshape.145) | copy-start | bytes 1924
  114.4 19.9 %copy-start.6 = (f32[4,10,128]{2,1,0:T(8,128)S(1)}, f32[4,10,128]{2,1,0:T(8,128)}, u32[]{:S(2)}) copy-start(f32[4,10,128]{2,1,0:T(8,128)} %copy-done.5) | copy-start | bytes 61444
  114.4 19.9 %copy-start.8 = (f32[4,10,128]{2,1,0:T(8,128)S(1)}, f32[4,10,128]{2,1,0:T(8,128)}, u32[]{:S(2)}) copy-start(f32[4,10,128]{2,1,0:T(8,128)} %copy-done.7) | copy-start | bytes 61444
  122.3 19.0 %collective-permute-start.7 = (f32[4,608]{1,0:T(4,128)S(1)}, f32[4,608]{1,0:T(4,128)S(1)}, u32[]{:S(2)}, u32[]{:S(2)}) collective-permute-start(f32[4,608]{1,0:T(4,128)S(1)} %reshape.132), channel_id=1, source_target_pairs={{1,120},{2,121},{3,122},{4,123},{5,124},{6,125},{7,126},{9,0},{10,... | collective-permute-start | bytes 29192 | tf_op jit(solution)/shard_map/ppermute | solution.py:36
  128.8 12.6 %collective-permute-start.3 = (f32[64,608]{0,1:T(8,128)S(1)}, f32[64,608]{0,1:T(8,128)S(1)}, u32[]{:S(2)}, u32[]{:S(2)}) collective-permute-start(f32[64,608]{0,1:T(8,128)S(1)} %bitcast.50), channel_id=1, source_target_pairs={{0,8},{8,16},{16,24},{24,32},{32,40},{40,48},{48,56},{56,64},{64,7... | collective-permute-start | bytes 466952 | tf_op jit(solution)/shard_map/ppermute | solution.py:18
  128.9 16.2 %collective-permute-start.4 = (f32[64,608]{0,1:T(8,128)S(1)}, f32[64,608]{0,1:T(8,128)}, u32[]{:S(2)}, u32[]{:S(2)}) collective-permute-start(f32[64,608]{0,1:T(8,128)S(1)} %bitcast.49), channel_id=1, source_target_pairs={{0,120},{8,0},{16,8},{24,16},{32,24},{40,32},{48,40},{56,48},{64,5... | collective-permute-start | bytes 466952 | tf_op jit(solution)/shard_map/ppermute | solution.py:18
  149.4 16.4 %copy-start.10 = (f32[152]{0:T(256)S(1)}, f32[152]{0:T(256)}, u32[]{:S(2)}) copy-start(f32[152]{0:T(256)} %fusion.15) | copy-start | bytes 1828

commit v2 on v1

--- a/solution.py
+++ b/solution.py
@@ -36,36 +36,74 @@
     return lax.ppermute(block, ("lon", "lat"), pairs)
 
 
-def with_halo(v):
-    rows, ch, cols = v.shape
-    r = RADIUS
-
-    def dense(a):
-        return a.reshape(a.shape[0], ch * r)
-
-    def back(a, n):
-        return a.reshape(n, ch, r)
-
-    west = back(shift_lon(dense(v[:, :, cols - r :]), 1), rows)
-    east = back(shift_lon(dense(v[:, :, :r]), -1), rows)
-    south = shift_lat(v[rows - r :], 1)
-    north = shift_lat(v[:r], -1)
-    sw = back(shift_both(dense(v[rows - r :, :, cols - r :]), 1, 1), r)
-    se = back(shift_both(dense(v[rows - r :, :, :r]), -1, 1), r)
-    nw = back(shift_both(dense(v[:r, :, cols - r :]), 1, -1), r)
-    ne = back(shift_both(dense(v[:r, :, :r]), -1, -1), r)
-    top = jnp.concatenate([sw, south, se], axis=2)
-    mid = jnp.concatenate([west, v, east], axis=2)
-    bot = jnp.concatenate([nw, north, ne], axis=2)
-    full = jnp.concatenate([top, mid, bot], axis=0)
-    return jnp.pad(full, ((0, 0), (0, 0), (0, LANES - cols - 2 * r)))
-
-
-def passes_kernel(p_ref, s_ref, lvl_ref, bal_ref, out_ref, a_ref, b_ref, u_ref):
+DIRECTIONS = (
+    ("west", lambda v, r: v[:, :, v.shape[2] - r :], "lon", 1, 0),
+    ("east", lambda v, r: v[:, :, :r], "lon", -1, 0),
+    ("south", lambda v, r: v[v.shape[0] - r :], "lat", 0, 1),
+    ("north", lambda v, r: v[:r], "lat", 0, -1),
+    ("sw", lambda v, r: v[v.shape[0] - r :, :, v.shape[2] - r :], "both", 1, 1),
+    ("se", lambda v, r: v[v.shape[0] - r :, :, :r], "both", -1, 1),
+    ("nw", lambda v, r: v[:r, :, v.shape[2] - r :], "both", 1, -1),
+    ("ne", lambda v, r: v[:r, :, :r], "both", -1, -1),
+)
+
+
+def exchange(parts):
+    got = [dict() for _ in parts]
+    for name, take, axis, step_lon, step_lat in DIRECTIONS:
+        pieces = [take(v, RADIUS) for v in parts]
+        flat = jnp.concatenate([p.reshape(-1) for p in pieces])
+        if axis == "lon":
+            flat = shift_lon(flat, step_lon)
+        elif axis == "lat":
+            flat = shift_lat(flat, step_lat)
+        else:
+            flat = shift_both(flat, step_lon, step_lat)
+        offset = 0
+        for i, p in enumerate(pieces):
+            got[i][name] = flat[offset : offset + p.size].reshape(p.shape)
+            offset += p.size
+    return got
+
+
+def side_lanes(east, west, gap):
+    zeros = jnp.zeros(east.shape[:2] + (gap,), jnp.float32)
+    return jnp.concatenate([east, zeros, west], axis=2)
+
+
+def assemble(v, h):
+    cols = v.shape[2]
+    gap = LANES - cols - 2 * RADIUS
+    top = jnp.concatenate([h["south"], side_lanes(h["se"], h["sw"], gap)], axis=2)
+    mid = jnp.concatenate([v, side_lanes(h["east"], h["west"], gap)], axis=2)
+    bot = jnp.concatenate([h["north"], side_lanes(h["ne"], h["nw"], gap)], axis=2)
+    return jnp.concatenate([top, mid, bot], axis=0)
+
+
+def split_bf16(x):
+    hi = x.astype(jnp.bfloat16)
+    lo = (x - hi.astype(jnp.float32)).astype(jnp.bfloat16)
+    return hi, lo
+
+
+def passes_kernel(
+    v_ref, ew_ref, top_ref, bot_ref, s_ref, lvl_ref, bal_ref, out_ref, a_ref, b_ref, p_ref, u_ref
+):
     full = p_ref.shape[0]
+    rows = v_ref.shape[0]
+    cols = v_ref.shape[2]
     chans = p_ref.shape[1]
     out_ch = out_ref.shape[1]
-    out_x = out_ref.shape[2]
+    p_ref[:RADIUS] = top_ref[...]
+    p_ref[full - RADIUS :] = bot_ref[...]
+
+    def fill(y, carry):
+        p_ref[y + RADIUS, :, :cols] = v_ref[y]
+        p_ref[y + RADIUS, :, cols:] = ew_ref[y]
+        return carry
+
+    lax.fori_loop(0, rows, fill, 0)
+    b_hi, b_lo = split_bf16(bal_ref[...])
     srcs = [p_ref, a_ref, b_ref, a_ref]
     dsts = [a_ref, b_ref, a_ref, None]
     for p in range(PASSES):
@@ -97,24 +135,26 @@
                 u_ref[c0 : c0 + CHUNK, :] = jnp.where(
                     lvl_ref[c0 : c0 + CHUNK, :] < depth, acc, 0.0
                 )
-            res = jnp.dot(
-                bal_ref[...],
-                u_ref[...],
-                precision=lax.Precision.HIGHEST,
-                preferred_element_type=jnp.float32,
-            )
+            u_hi, u_lo = split_bf16(u_ref[...])
+            res = jnp.dot(b_hi, u_hi, preferred_element_type=jnp.float32)
+            res = res + jnp.dot(b_hi, u_lo, preferred_element_type=jnp.float32)
+            res = res + jnp.dot(b_lo, u_hi, preferred_element_type=jnp.float32)
             if dst is None:
-                shifted = pltpu.roll(res, LANES - RADIUS, 1)
-                out_ref[y - RADIUS] = shifted[:out_ch, :out_x]
+                out_ref[y - RADIUS] = res[:out_ch, :cols]
             else:
                 dst[y] = res
             return carry
 
-        lax.fori_loop(p + 1, full - 1 - p, row, 0)
-
-
-def run_passes(padded, stat, balance, rows, chans, cols):
-    full = padded.shape[0]
+        lax.fori_loop(p + 1, full - 1 - p, row, 0, unroll=2)
+
+
+def run_passes(field, halos, stat, balance, chans):
+    rows, cpad, cols = field.shape
+    full = rows + 2 * RADIUS
+    gap = LANES - cols - 2 * RADIUS
+    ew = side_lanes(halos["east"], halos["west"], gap)
+    top = jnp.concatenate([halos["south"], side_lanes(halos["se"], halos["sw"], gap)], axis=2)
+    bot = jnp.concatenate([halos["north"], side_lanes(halos["ne"], halos["nw"], gap)], axis=2)
     lvl = jnp.broadcast_to(
         (jnp.arange(CPAD) % LEVELS).astype(jnp.float32)[:, None], (CPAD, LANES)
     )
@@ -124,20 +164,21 @@
     return pl.pallas_call(
         passes_kernel,
         out_shape=jax.ShapeDtypeStruct((rows, chans, cols), jnp.float32),
-        in_specs=[pl.BlockSpec(memory_space=vmem)] * 4,
+        in_specs=[pl.BlockSpec(memory_space=vmem)] * 7,
         out_specs=pl.BlockSpec(memory_space=vmem),
         scratch_shapes=[
-            vmem(padded.shape, jnp.float32),
-            vmem(padded.shape, jnp.float32),
+            vmem((full, CPAD, LANES), jnp.float32),
+            vmem((full, CPAD, LANES), jnp.float32),
+            vmem((full, CPAD, LANES), jnp.float32),
             vmem((CPAD, LANES), jnp.float32),
         ],
         compiler_params=pltpu.CompilerParams(vmem_limit_bytes=62 * 1024 * 1024),
         cost_estimate=pl.CostEstimate(
-            flops=PASSES * (work * 20 + 2 * full * CPAD * CPAD * LANES),
+            flops=PASSES * (work * 20 + 6 * full * CPAD * CPAD * LANES),
             bytes_accessed=4 * (work + rows * chans * cols),
             transcendentals=0,
         ),
-    )(padded, stat, lvl, bal_t)
+    )(field, ew, top, bot, stat, lvl, bal_t)
 
 
 def local(innovations, owner_tile, obs_column, obs_depth, coefficients, sea_depth, balance):
@@ -149,7 +190,7 @@
     cols_x = sea_depth.shape[1]
 
     stat = jnp.concatenate([coefficients, sea_depth.astype(jnp.float32)[None]], axis=0)
-    stat = with_halo(jnp.transpose(stat, (1, 0, 2)))
+    stat = jnp.transpose(stat, (1, 0, 2))
 
     level_ids = jnp.arange(channels) % LEVELS
     kept = jnp.where(level_ids[:, None] < obs_depth[None, :], innovations, 0.0)
@@ -167,8 +208,9 @@
     field = jnp.zeros((rows_y * cols_x, channels), jnp.float32).at[where].add(got[:, :channels])
     field = jnp.transpose(field.reshape(rows_y, cols_x, channels), (0, 2, 1))
     field = jnp.pad(field, ((0, 0), (0, CPAD - channels), (0, 0)))
-    padded = with_halo(field)
-    out = run_passes(padded, stat, balance, rows_y, channels, cols_x)
+    field_halo, stat_halo = exchange([field, stat])
+    stat = assemble(stat, stat_halo)
+    out = run_passes(field, field_halo, stat, balance, channels)
     return jnp.transpose(out, (1, 0, 2))
 
 

time: 300 us -> 247 us (0.82)
  Pallas kernels: 126 us -> 83.1 us
  starting transfers between devices: 68.3 us -> 37.1 us
  waiting for transfers between devices: 2.27 us -> 24.5 us
  other arithmetic: 39.7 us -> 30.7 us
  local copies, waits for them, and re-layouts: 61.5 us -> 69.8 us
    pallas_call x1, Pallas kernels: 126 us -> 83.1 us  [run_passes(): pl.pallas_call(passes_kernel, out_shape=jax.ShapeDtypeStruct((rows, chans...]
    all_to_all x1, waiting for transfers between devices: 0.01 us -> 24.4 us  [local(): lax.all_to_all(send.reshape(devices, capacity, channels + 1), ('lon', 'la...]
    ppermute x8 -> x4, starting transfers between devices: 34.4 us -> 12.6 us  [shift_both(): return lax.ppermute(block, ('lon', 'lat'), pairs)]
    reshape x20 -> x28, local copies, waits for them, and re-layouts: 12.6 us -> 28.4 us  [the longest x14 15.2 us: exchange(): got[i][name] = flat[offset:offset + p.size].reshape(p.shape)]
    slice x10 -> x18, local copies, waits for them, and re-layouts: 22.5 us -> 13.3 us  [the longest x2 6.23 us: v[:, :, :r]]
    concatenate x2 -> x11, other arithmetic: 17.9 us -> 11 us  [the longest x1 7.52 us: side_lanes(): return jnp.concatenate([east, zeros, west], axis=2)]
    ppermute x4 -> x2, starting transfers between devices: 12.8 us -> 5.85 us  [shift_lat(): lax.ppermute(block, 'lat', [(i, i + step) for i in range(count) if 0 <= i...]
    ppermute x4 -> x2, starting transfers between devices: 11 us -> 8.46 us  [shift_lon(): lax.ppermute(block, 'lon', [(i, (i + step) % count) for i in range(count)])]
  transfers between devices with their start and end apart: 17 -> 9, of which waited for: 1 -> 1; matrix products, arithmetic and copies ran while one was open for 23% -> 19% of each run, Pallas kernels for 0% -> 0%
where the time goes in v2:
time: 247 us; the launch traced here: 246 us
  Pallas kernels  83.1 us (34%)
  local copies, waits for them, and re-layouts  69.8 us (28%)
  starting transfers between devices  37.1 us (15%)
  other arithmetic  30.7 us (12%)
  waiting for transfers between devices  24.5 us (10%)
    pallas_call x1, Pallas kernels, run_passes(): pl.pallas_call(passes_kernel, out_shape=jax.ShapeDtypeStruct((rows, chans...  83.1 us
    all_to_all x1, waiting for transfers between devices, local(): lax.all_to_all(send.reshape(devices, capacity, channels + 1), ('lon', 'la...  24.4 us
    scatter-add x1, other arithmetic, local(): jnp.zeros((rows_y * cols_x, channels), jnp.float32).at[where]  15.4 us
    reshape x14, local copies, waits for them, and re-layouts, exchange(): got[i][name] = flat[offset:offset + p.size].reshape(p.shape)  15.2 us
    reshape x14, local copies, waits for them, and re-layouts, exchange(): flat = jnp.concatenate([p.reshape(-1) for p in pieces])  13.2 us
    ppermute x4, starting transfers between devices, shift_both(): return lax.ppermute(block, ('lon', 'lat'), pairs)  12.6 us
    all_to_all x1, starting transfers between devices, local(): lax.all_to_all(send.reshape(devices, capacity, channels + 1), ('lon', 'la...  10.2 us
    ppermute x2, starting transfers between devices, shift_lon(): lax.ppermute(block, 'lon', [(i, (i + step) % count) for i in range(count)])  8.46 us
  transfers between devices with their start and end apart: 9, of which 1 were waited for; matrix products, arithmetic and copies ran while one was open for 19% of the time, Pallas kernels for 0%

profile of v2, /device:TPU:34, one launch (start us, length us, event | category | flops | bytes accessed | tf_op | source)
XLA Modules:
  0.0 245.5 jit_solution(8586531239205178296)
XLA Ops:
  0.0 0.8 copy.20
  1.1 0.9 fusion.7
  2.0 0.7 compare_select_fusion.1
  2.7 0.7 convert_element_type.30
  3.4 1.1 select_bitcast_fusion
  4.7 3.6 %scatter_custom_fusion = f32[2048,151]{1,0:T(8,128)} fusion(s32[512]{0:T(512)S(1)} %bitcast.63, f32[512,151]{1,0:T(8,128)S(1)} %copy.22, f32[]{:T(128)} %constant.13.clone.1), kind=kCustom, calls=%fused_computation.10 | custom fusion | bytes 1236996 | tf_op jit(solution)/shard_map/scatter | solution.py:203
  8.4 10.2 %all-to-all-start = ((f32[128,16,151]{2,1,0:T(8,128)}), f32[128,16,151]{2,1,0:T(8,128)S(1)}, u32[]{:S(2)}, u32[]{:S(2)}) async-start(f32[128,16,151]{2,1,0:T(8,128)} %bitcast.44), calls=%async_computation | async-start | bytes 4194304 | tf_op jit(solution)/shard_map/all_to_all | solution.py:204
  19.5 0.9 fusion.14
  20.5 1.2 reshape.147
  22.1 0.7 pad.9.bal_ref
  22.8 24.4 %all-to-all-done = f32[128,16,151]{2,1,0:T(8,128)S(1)} async-done(((f32[128,16,151]{2,1,0:T(8,128)}), f32[128,16,151]{2,1,0:T(8,128)S(1)}, u32[]{:S(2)}, u32[]{:S(2)}) %all-to-all-start) | async-done | bytes 1237024 | tf_op jit(solution)/shard_map/all_to_all | solution.py:204
  47.2 0.6 fusion.3
  47.9 15.4 %scatter_custom_fusion.1 = f32[8192,150]{1,0:T(8,128)} fusion(s32[2048]{0:T(1024)S(1)} %fusion.3, f32[]{:T(128)} %constant.13.clone.1, f32[2048,151]{1,0:T(8,128)S(1)} %bitcast.43), kind=kCustom, calls=%fused_computation.3 | custom fusion | flops 307200 | bytes 7012356 | tf_op jit(solution)/shard_map/scatter-add | solution.py:208
  63.2 8.3 %copy.24 = f32[64,128,150]{1,2,0:T(8,128)} copy(f32[64,128,150]{2,1,0:T(8,128)} %bitcast.41) | data formatting | bytes 9830400 | tf_op jit(solution)/shard_map/reshape | solution.py:209
  71.6 1.6 pad_slice_fusion.1
  73.2 1.2 copy-done
  74.3 5.3 %pad_slice_fusion.7 = (f32[64,152,4]{2,1,0:T(8,128)}, f32[64,152,4]{2,1,0:T(8,128)}) fusion(f32[64,150,128]{2,1,0:T(8,128)S(1)} %bitcast.39), kind=kLoop, calls=%fused_computation.46 | loop fusion | bytes 5226496 | tf_op jit(solution)/shard_map/slice | solution.py:41
  79.9 2.7 %collective-permute-start.3 = (f32[2592]{0:T(1024)S(1)}, f32[2592]{0:T(1024)S(1)}, u32[]{:S(2)}, u32[]{:S(2)}) collective-permute-start(f32[2592]{0:T(1024)S(1)} %pad_maximum_fusion.8), channel_id=1, source_target_pairs={{0,121},{1,122},{2,123},{3,124},{4,125},{5,126},{6,127},{8,1},{9,2... | collective-permute-start | bytes 31112 | tf_op jit(solution)/shard_map/ppermute | solution.py:36
  82.8 3.0 %collective-permute-start.4 = (f32[2592]{0:T(1024)S(1)}, f32[2592]{0:T(1024)S(1)}, u32[]{:S(2)}, u32[]{:S(2)}) collective-permute-start(f32[2592]{0:T(1024)S(1)} %pad_maximum_fusion.9), channel_id=1, source_target_pairs={{0,9},{1,10},{2,11},{3,12},{4,13},{5,14},{6,15},{8,17},{9,18},{10,... | collective-permute-start | bytes 31112 | tf_op jit(solution)/shard_map/ppermute | solution.py:36
  86.1 4.6 %collective-permute-start.6 = (f32[2592]{0:T(1024)S(1)}, f32[2592]{0:T(1024)S(1)}, u32[]{:S(2)}, u32[]{:S(2)}) collective-permute-start(f32[2592]{0:T(1024)S(1)} %pad_maximum_fusion.10), channel_id=1, source_target_pairs={{1,120},{2,121},{3,122},{4,123},{5,124},{6,125},{7,126},{9,0},{10,... | collective-permute-start | bytes 31112 | tf_op jit(solution)/shard_map/ppermute | solution.py:36
  90.9 2.2 collective-permute-start.7
  93.1 5.3 %reshape.146 = f32[38912]{0:T(1024)S(1)} reshape(f32[64,152,4]{2,1,0:T(8,128)} %get-tuple-element.11) | data formatting | bytes 311296 | tf_op jit(solution)/shard_map/reshape | solution.py:55
  98.4 8.4 %collective-permute-start = (f32[41472]{0:T(1024)S(1)}, f32[41472]{0:T(1024)S(1)}, u32[]{:S(2)}, u32[]{:S(2)}) collective-permute-start(f32[41472]{0:T(1024)S(1)} %pad_maximum_fusion.6), channel_id=1, source_target_pairs={{0,120},{8,0},{16,8},{24,16},{32,24},{40,32},{48,40},{56,48},{64,5... | collective-permute-start | bytes 497672 | tf_op jit(solution)/shard_map/ppermute | solution.py:18
  106.8 5.3 %reshape.149 = f32[38912]{0:T(1024)S(1)} reshape(f32[64,152,4]{2,1,0:T(8,128)} %get-tuple-element.12) | data formatting | bytes 311296 | tf_op jit(solution)/shard_map/reshape | solution.py:55
  112.3 0.7 pad_maximum_fusion.4
  113.1 5.0 %pad.8.v_ref = f32[64,152,128]{2,1,0:T(8,128)} pad(f32[64,150,128]{2,1,0:T(8,128)} %bitcast.38, f32[]{:T(128)} %constant.13.clone.1), padding=0_0x0_2x0_0 | pad | bytes 9895940 | tf_op jit(solution)/shard_map/jit(_pad)/pad | solution.py:210
  118.1 1.9 collective-permute-start.2
  120.2 3.9 %collective-permute-start.5 = (f32[82944]{0:T(1024)}, f32[82944]{0:T(1024)}, u32[]{:S(2)}, u32[]{:S(2)}) collective-permute-start(f32[82944]{0:T(1024)} %pad_maximum_fusion.4), channel_id=1, source_target_pairs={{1,0},{2,1},{3,2},{4,3},{5,4},{6,5},{7,6},{9,8},{10,9},{11,10},{12... | collective-permute-start | bytes 995336 | tf_op jit(solution)/shard_map/ppermute | solution.py:23
  124.4 0.3 reshape.157
  124.7 0.3 reshape.160
  125.0 0.3 reshape.166
  125.3 0.3 reshape.169
  125.7 0.6 copy-done.2
  126.5 0.7 copy-done.3
  127.4 0.9 slice.148
  128.3 6.6 %reshape.148 = f32[64,152,4]{2,1,0:T(8,128)} reshape(f32[38912]{0:T(1024)S(1)} %slice.148) | data formatting | bytes 311296 | tf_op jit(solution)/shard_map/reshape | solution.py:64
  134.9 0.9 slice.150
  135.9 6.6 %reshape.151 = f32[64,152,4]{2,1,0:T(8,128)} reshape(f32[38912]{0:T(1024)S(1)} %slice.150) | data formatting | bytes 311296 | tf_op jit(solution)/shard_map/reshape | solution.py:64
  142.5 7.5 %pad_maximum_fusion.ew_ref = f32[64,152,128]{2,1,0:T(8,128)} fusion(f32[64,152,4]{2,1,0:T(8,128)} %reshape.151, f32[64,152,4]{2,1,0:T(8,128)} %reshape.148, f32[128]{0:T(128)S(1)} %pad.43.clone), kind=kLoop, calls=%fused_computation.2 | loop fusion | flops 2490368 | bytes 5292544 | tf_op jit(solution)/shard_map/concatenate | solution.py:71
  150.0 0.7 slice.163
  150.7 0.7 slice.168
  151.5 1.0 slice.152
  152.5 1.0 slice.158
  153.5 1.3 pad_maximum_fusion.2
  154.8 1.3 maximum_maximum_fusion.s_ref
  156.1 0.8 broadcast_in_dim.40.lvl_ref
  156.8 83.1 %shard_map.73 = f32[64,150,128]{2,1,0:T(8,128)} custom-call(f32[64,152,128]{2,1,0:T(8,128)} %pad.8.v_ref, f32[64,152,128]{2,1,0:T(8,128)} %pad_maximum_fusion.ew_ref, f32[4,152,256]{2,1,0:T(8,128)} %get-tuple-element.22.top_ref, f32[4,152,256]{2,1,0:T(8,128)} %get-tuple-element.21.bot_ref, f32[72,10,256]{2,1,0:T(8,128)} %maximum_maximum_fusion.s_ref, ...), custom_call_target="tpu_custom_call" | custom-call | flops 10444603392 | bytes 16121856 | tf_op jit(solution)/shard_map/pallas_call | solution.py:164
  239.9 5.6 %copy.27 = f32[150,64,128]{2,1,0:T(8,128)} copy(f32[150,64,128]{2,0,1:T(8,128)} %bitcast.45) | data formatting | bytes 9830400 | tf_op jit(solution)/shard_map/transpose | solution.py:214
  (74 shorter events, 3.5 us)
Async XLA Ops:
  8.4 10.4 %copy-start.1 = (f32[9,64,128]{2,1,0:T(8,128)S(1)}, f32[9,64,128]{2,1,0:T(8,128)}, u32[]{:S(2)}) copy-start(f32[9,64,128]{2,1,0:T(8,128)} %param.11) | copy-start | bytes 884740
  8.4 10.6 %copy-start.5 = (s32[64,128]{1,0:T(8,128)S(1)}, s32[64,128]{1,0:T(8,128)}, u32[]{:S(2)}) copy-start(s32[64,128]{1,0:T(8,128)} %param.12) | copy-start | bytes 98308
  8.4 38.9 %all-to-all-start = ((f32[128,16,151]{2,1,0:T(8,128)}), f32[128,16,151]{2,1,0:T(8,128)S(1)}, u32[]{:S(2)}, u32[]{:S(2)}) async-start(f32[128,16,151]{2,1,0:T(8,128)} %bitcast.44), calls=%async_computation | async-start | bytes 4194304 | tf_op jit(solution)/shard_map/all_to_all | solution.py:204
  19.0 3.0 %copy-start.4 = (f32[150,150]{1,0:T(8,128)S(1)}, f32[150,150]{1,0:T(8,128)}, u32[]{:S(2)}) copy-start(f32[150,150]{1,0:T(8,128)} %param.13) | copy-start | bytes 270004
  71.6 2.8 %copy-start = (f32[64,128,150]{1,2,0:T(8,128)S(1)}, f32[64,128,150]{1,2,0:T(8,128)}, u32[]{:S(2)}) copy-start(f32[64,128,150]{1,2,0:T(8,128)} %copy.24) | copy-start | bytes 14745604
  79.9 32.3 %collective-permute-start.3 = (f32[2592]{0:T(1024)S(1)}, f32[2592]{0:T(1024)S(1)}, u32[]{:S(2)}, u32[]{:S(2)}) collective-permute-start(f32[2592]{0:T(1024)S(1)} %pad_maximum_fusion.8), channel_id=1, source_target_pairs={{0,121},{1,122},{2,123},{3,124},{4,125},{5,126},{6,127},{8,1},{9,2... | collective-permute-start | bytes 31112 | tf_op jit(solution)/shard_map/ppermute | solution.py:36
  82.8 35.3 %collective-permute-start.4 = (f32[2592]{0:T(1024)S(1)}, f32[2592]{0:T(1024)S(1)}, u32[]{:S(2)}, u32[]{:S(2)}) collective-permute-start(f32[2592]{0:T(1024)S(1)} %pad_maximum_fusion.9), channel_id=1, source_target_pairs={{0,9},{1,10},{2,11},{3,12},{4,13},{5,14},{6,15},{8,17},{9,18},{10,... | collective-permute-start | bytes 31112 | tf_op jit(solution)/shard_map/ppermute | solution.py:36
  86.1 34.1 %collective-permute-start.6 = (f32[2592]{0:T(1024)S(1)}, f32[2592]{0:T(1024)S(1)}, u32[]{:S(2)}, u32[]{:S(2)}) collective-permute-start(f32[2592]{0:T(1024)S(1)} %pad_maximum_fusion.10), channel_id=1, source_target_pairs={{1,120},{2,121},{3,122},{4,123},{5,124},{6,125},{7,126},{9,0},{10,... | collective-permute-start | bytes 31112 | tf_op jit(solution)/shard_map/ppermute | solution.py:36
  90.9 33.3 %collective-permute-start.7 = (f32[2592]{0:T(1024)S(1)}, f32[2592]{0:T(1024)S(1)}, u32[]{:S(2)}, u32[]{:S(2)}) collective-permute-start(f32[2592]{0:T(1024)S(1)} %pad_maximum_fusion.11), channel_id=1, source_target_pairs={{1,8},{2,9},{3,10},{4,11},{5,12},{6,13},{7,14},{9,16},{10,17},{11,... | collective-permute-start | bytes 31112 | tf_op jit(solution)/shard_map/ppermute | solution.py:36
  98.4 27.2 %collective-permute-start = (f32[41472]{0:T(1024)S(1)}, f32[41472]{0:T(1024)S(1)}, u32[]{:S(2)}, u32[]{:S(2)}) collective-permute-start(f32[41472]{0:T(1024)S(1)} %pad_maximum_fusion.6), channel_id=1, source_target_pairs={{0,120},{8,0},{16,8},{24,16},{32,24},{40,32},{48,40},{56,48},{64,5... | collective-permute-start | bytes 497672 | tf_op jit(solution)/shard_map/ppermute | solution.py:18
  112.2 14.3 %collective-permute-start.1 = (f32[41472]{0:T(1024)S(1)}, f32[41472]{0:T(1024)S(1)}, u32[]{:S(2)}, u32[]{:S(2)}) collective-permute-start(f32[41472]{0:T(1024)S(1)} %pad_maximum_fusion.7), channel_id=1, source_target_pairs={{0,8},{8,16},{16,24},{24,32},{32,40},{40,48},{48,56},{56,64},{64,7... | collective-permute-start | bytes 497672 | tf_op jit(solution)/shard_map/ppermute | solution.py:18
  118.1 31.9 %collective-permute-start.2 = (f32[82944]{0:T(1024)S(1)}, f32[82944]{0:T(1024)}, u32[]{:S(2)}, u32[]{:S(2)}) collective-permute-start(f32[82944]{0:T(1024)S(1)} %pad_maximum_fusion.3), channel_id=1, source_target_pairs={{0,1},{1,2},{2,3},{3,4},{4,5},{5,6},{6,7},{8,9},{9,10},{10,11},{11... | collective-permute-start | bytes 995336 | tf_op jit(solution)/shard_map/ppermute | solution.py:23
  120.2 30.5 %collective-permute-start.5 = (f32[82944]{0:T(1024)}, f32[82944]{0:T(1024)}, u32[]{:S(2)}, u32[]{:S(2)}) collective-permute-start(f32[82944]{0:T(1024)} %pad_maximum_fusion.4), channel_id=1, source_target_pairs={{1,0},{2,1},{3,2},{4,3},{5,4},{6,5},{7,6},{9,8},{10,9},{11,10},{12... | collective-permute-start | bytes 995336 | tf_op jit(solution)/shard_map/ppermute | solution.py:23
  125.7 0.7 copy-start.2
  126.5 0.7 copy-start.3

commit v3 on v2

--- a/solution.py
+++ b/solution.py
@@ -64,6 +64,27 @@
             got[i][name] = flat[offset : offset + p.size].reshape(p.shape)
             offset += p.size
     return got
+
+
+def field_halos(f):
+    rows, cols, _ = f.shape
+    r = RADIUS
+    v_top = jnp.transpose(f[:r], (0, 2, 1))
+    v_bot = jnp.transpose(f[rows - r :], (0, 2, 1))
+
+    def t(a):
+        return jnp.transpose(a, (0, 2, 1))
+
+    return {
+        "west": t(shift_lon(f[:, cols - r :, :], 1)),
+        "east": t(shift_lon(f[:, :r, :], -1)),
+        "south": shift_lat(v_bot, 1),
+        "north": shift_lat(v_top, -1),
+        "sw": t(shift_both(f[rows - r :, cols - r :, :], 1, 1)),
+        "se": t(shift_both(f[rows - r :, :r, :], -1, 1)),
+        "nw": t(shift_both(f[:r, cols - r :, :], 1, -1)),
+        "ne": t(shift_both(f[:r, :r, :], -1, -1)),
+    }
 
 
 def side_lanes(east, west, gap):
@@ -148,7 +169,8 @@
         lax.fori_loop(p + 1, full - 1 - p, row, 0, unroll=2)
 
 
-def run_passes(field, halos, stat, balance, chans):
+def run_passes(field_pm, halos, stat, balance, chans):
+    field = jnp.transpose(field_pm, (0, 2, 1))
     rows, cpad, cols = field.shape
     full = rows + 2 * RADIUS
     gap = LANES - cols - 2 * RADIUS
@@ -199,18 +221,24 @@
     before = jnp.cumsum(one_hot, axis=0) - one_hot
     slot_rank = jnp.sum(before * one_hot, axis=1)
     destination = targets * capacity + slot_rank
-    payload = jnp.concatenate([kept.T, obs_column.astype(jnp.float32)[:, None]], axis=1)
-    send = jnp.zeros((devices * capacity, channels + 1), jnp.float32).at[destination].set(payload)
+    payload = jnp.concatenate(
+        [
+            kept.T,
+            jnp.zeros((obs_count, CPAD - channels - 1), jnp.float32),
+            obs_column.astype(jnp.float32)[:, None],
+        ],
+        axis=1,
+    )
+    send = jnp.zeros((devices * capacity, CPAD), jnp.float32).at[destination].set(payload)
     got = lax.all_to_all(
-        send.reshape(devices, capacity, channels + 1), ("lon", "lat"), 0, 0, tiled=True
-    ).reshape(devices * capacity, channels + 1)
-    where = got[:, channels].astype(jnp.int32)
-    field = jnp.zeros((rows_y * cols_x, channels), jnp.float32).at[where].add(got[:, :channels])
-    field = jnp.transpose(field.reshape(rows_y, cols_x, channels), (0, 2, 1))
-    field = jnp.pad(field, ((0, 0), (0, CPAD - channels), (0, 0)))
-    field_halo, stat_halo = exchange([field, stat])
+        send.reshape(devices, capacity, CPAD), ("lon", "lat"), 0, 0, tiled=True
+    ).reshape(devices * capacity, CPAD)
+    where = got[:, CPAD - 1].astype(jnp.int32)
+    field = jnp.zeros((rows_y * cols_x, CPAD), jnp.float32).at[where].add(got)
+    field = field.reshape(rows_y, cols_x, CPAD)
+    (stat_halo,) = exchange([stat])
     stat = assemble(stat, stat_halo)
-    out = run_passes(field, field_halo, stat, balance, channels)
+    out = run_passes(field, field_halos(field), stat, balance, channels)
     return jnp.transpose(out, (1, 0, 2))
 
 

time: 247 us -> 223 us (0.903)
  local copies, waits for them, and re-layouts: 69.8 us -> 38.9 us
  starting transfers between devices: 37.1 us -> 62.3 us
  waiting for transfers between devices: 24.5 us -> 3.27 us
  other arithmetic: 30.7 us -> 33.3 us
    all_to_all x1, waiting for transfers between devices: 24.4 us -> 0.01 us  [local(): lax.all_to_all(send.reshape(devices, capacity, CPAD), ('lon', 'lat'), 0,...]
    ppermute x4 -> x8, starting transfers between devices: 12.6 us -> 31 us  [shift_both(): return lax.ppermute(block, ('lon', 'lat'), pairs)]
    reshape x14 -> x8, local copies, waits for them, and re-layouts: 15.2 us -> 1.52 us  [exchange(): got[i][name] = flat[offset:offset + p.size].reshape(p.shape)]
    reshape x14 -> x8, local copies, waits for them, and re-layouts: 13.2 us -> 1.79 us  [exchange(): flat = jnp.concatenate([p.reshape(-1) for p in pieces])]
    ppermute x0 -> x2, local copies, waits for them, and re-layouts: none -> 8.06 us  [shift_lon(): lax.ppermute(block, 'lon', [(i, (i + step) % count) for i in range(count)])]
    ppermute x2 -> x4, starting transfers between devices: 5.85 us -> 13.3 us  [shift_lat(): lax.ppermute(block, 'lat', [(i, i + step) for i in range(count) if 0 <= i...]
    slice x2 -> x1, local copies, waits for them, and re-layouts: 6.23 us -> 0.93 us  [v[:, :, :r]]
    pad x1 -> x0, local copies, waits for them, and re-layouts: 4.95 us -> none  [local(): field = jnp.pad(field, ((0, 0), (0, CPAD - channels), (0, 0)))]
  transfers between devices with their start and end apart: 9 -> 17, of which waited for: 1 -> 2; matrix products, arithmetic and copies ran while one was open for 19% -> 12% of each run, Pallas kernels for 0% -> 0%
where the time goes in v3:
time: 223 us; the launch traced here: 221 us
  Pallas kernels  82.9 us (37%)
  starting transfers between devices  62.3 us (28%)
  local copies, waits for them, and re-layouts  38.9 us (17%)
  other arithmetic  33.3 us (15%)
  waiting for transfers between devices  3.27 us (1%)
    pallas_call x1, Pallas kernels, run_passes(): pl.pallas_call(passes_kernel, out_shape=jax.ShapeDtypeStruct((rows, chans...  82.9 us
    ppermute x8, starting transfers between devices, shift_both(): return lax.ppermute(block, ('lon', 'lat'), pairs)  31 us
    scatter-add x1, other arithmetic, local(): field = jnp.zeros((rows_y * cols_x, CPAD), jnp.float32).at[where].add(got)  16.7 us
    ppermute x4, starting transfers between devices, shift_lat(): lax.ppermute(block, 'lat', [(i, i + step) for i in range(count) if 0 <= i...  13.3 us
    all_to_all x1, starting transfers between devices, local(): lax.all_to_all(send.reshape(devices, capacity, CPAD), ('lon', 'lat'), 0,...  10.2 us
    reshape x1, local copies, waits for them, and re-layouts, local(): field = field.reshape(rows_y, cols_x, CPAD)  8.26 us
    ppermute x2, local copies, waits for them, and re-layouts, shift_lon(): lax.ppermute(block, 'lon', [(i, (i + step) % count) for i in range(count)])  8.06 us
    ppermute x4, starting transfers between devices, shift_lon(): lax.ppermute(block, 'lon', [(i, (i + step) % count) for i in range(count)])  7.78 us
  transfers between devices with their start and end apart: 17, of which 2 were waited for; matrix products, arithmetic and copies ran while one was open for 12% of the time, Pallas kernels for 0%

profile of v3, /device:TPU:34, one launch (start us, length us, event | category | flops | bytes accessed | tf_op | source)
XLA Modules:
  0.0 221.0 jit_solution(9896304448270908130)
XLA Ops:
  0.0 0.8 copy.46
  0.8 0.2 fusion.7
  1.1 0.9 fusion.6
  2.0 0.7 compare_select_fusion.1
  2.7 0.7 convert_element_type.28
  3.5 1.1 select_bitcast_fusion
  4.6 0.2 copy.48
  4.8 3.6 %scatter_custom_fusion = f32[2048,152]{1,0:T(8,128)} fusion(s32[512]{0:T(512)S(1)} %bitcast.65, f32[512,152]{1,0:T(8,128)S(1)} %copy.48, f32[]{:T(128)} %constant.13.clone.1), kind=kCustom, calls=%fused_computation.9 | custom fusion | bytes 1245188 | tf_op jit(solution)/shard_map/scatter | solution.py:232
  8.5 10.2 %all-to-all-start = ((f32[128,16,152]{2,1,0:T(8,128)}), f32[128,16,152]{2,1,0:T(8,128)S(1)}, u32[]{:S(2)}, u32[]{:S(2)}) async-start(f32[128,16,152]{2,1,0:T(8,128)} %bitcast.9), calls=%async_computation | async-start | bytes 4194304 | tf_op jit(solution)/shard_map/all_to_all | solution.py:233
  18.7 0.2 copy.63
  19.2 6.6 %collective-permute-start.9 = (f32[160]{0:T(256)S(1)}, f32[160]{0:T(256)S(1)}, u32[]{:S(2)}, u32[]{:S(2)}) collective-permute-start(f32[160]{0:T(256)S(1)} %reshape.102), channel_id=1, source_target_pairs={{0,121},{1,122},{2,123},{3,124},{4,125},{5,126},{6,127},{8,1},{9,2... | collective-permute-start | bytes 1928 | tf_op jit(solution)/shard_map/ppermute | solution.py:36
  25.9 1.9 collective-permute-start.10
  28.0 5.8 %collective-permute-start.14 = (f32[160]{0:T(256)S(1)}, f32[160]{0:T(256)S(1)}, u32[]{:S(2)}, u32[]{:S(2)}) collective-permute-start(f32[160]{0:T(256)S(1)} %reshape.112), channel_id=1, source_target_pairs={{1,120},{2,121},{3,122},{4,123},{5,124},{6,125},{7,126},{9,0},{10,... | collective-permute-start | bytes 1928 | tf_op jit(solution)/shard_map/ppermute | solution.py:36
  33.8 1.9 collective-permute-start.15
  35.7 0.9 fusion.16
  36.7 1.2 reshape.106
  37.9 7.2 %collective-permute-start.11 = (f32[2560]{0:T(1024)S(1)}, f32[2560]{0:T(1024)S(1)}, u32[]{:S(2)}, u32[]{:S(2)}) collective-permute-start(f32[2560]{0:T(1024)S(1)} %reshape.106), channel_id=1, source_target_pairs={{0,120},{8,0},{16,8},{24,16},{32,24},{40,32},{48,40},{56,48},{64,5... | collective-permute-start | bytes 30728 | tf_op jit(solution)/shard_map/ppermute | solution.py:18
  45.4 4.4 %collective-permute-start.8 = (f32[5120]{0:T(1024)S(1)}, f32[5120]{0:T(1024)S(1)}, u32[]{:S(2)}, u32[]{:S(2)}) collective-permute-start(f32[5120]{0:T(1024)S(1)} %reshape.100), channel_id=1, source_target_pairs={{0,1},{1,2},{2,3},{3,4},{4,5},{5,6},{6,7},{8,9},{9,10},{10,11},{11... | collective-permute-start | bytes 61448 | tf_op jit(solution)/shard_map/ppermute | solution.py:23
  49.8 1.9 collective-permute-start.13
  52.1 0.7 pad.4.bal_ref
  53.4 1.0 reshape.109
  54.3 2.0 collective-permute-done.13
  56.4 2.4 %maximum_maximum_fusion.s_ref = f32[72,10,256]{2,1,0:T(8,128)} fusion(f32[4,10,4]{2,1,0:T(8,128)S(1)} %reshape.115, f32[4,10,120]{2,1,0:T(8,128)S(1)} %broadcast.67, f32[4,10,4]{2,1,0:T(8,128)S(1)} %reshape.113, f32[4,10,128]{2,1,0:T(8,128)S(1)} %reshape.111, f32[64,10,4]{2,1,0:T(8,128)} %reshape.109, f32[64,10,4]{2,1,0:T(8,128)S(1)} %reshape.107, ...), kind=kLoop, calls=%fused_computation.6 | loop fusion | flops 2027520 | bytes 1221888 | tf_op jit(solution)/shard_map/concatenate | solution.py:101
  58.7 0.6 fusion.2
  59.4 16.7 %scatter_custom_fusion.1 = f32[8192,152]{1,0:T(8,128)} fusion(s32[2048]{0:T(1024)S(1)} %fusion.2, f32[2048,152]{1,0:T(8,128)S(1)} %bitcast.47, f32[]{:T(128)} %constant.13.clone.1), kind=kCustom, calls=%fused_computation.3 | custom fusion | flops 311296 | bytes 4980740 | tf_op jit(solution)/shard_map/scatter-add | solution.py:237
  76.0 8.3 %copy.50 = f32[64,128,152]{1,2,0:T(8,128)} copy(f32[64,128,152]{2,1,0:T(8,128)} %bitcast.40) | data formatting | bytes 9961472 | tf_op jit(solution)/shard_map/reshape | solution.py:238
  84.3 1.3 fusion.12
  85.6 1.5 fusion.13
  87.1 4.0 %collective-permute-start.3 = (f32[4,4,152]{1,2,0:T(8,128)S(1)}, f32[4,4,152]{1,2,0:T(8,128)S(1)}, u32[]{:S(2)}, u32[]{:S(2)}) collective-permute-start(f32[4,4,152]{1,2,0:T(8,128)S(1)} %get-tuple-element.12), channel_id=1, source_target_pairs={{0,121},{1,122},{2,123},{3,124},{4,125},{5,126},{6,127},{8,1},{9,2... | collective-permute-start | bytes 29192 | tf_op jit(solution)/shard_map/ppermute | solution.py:36
  91.1 0.8 copy.51
  91.9 0.8 copy.53
  92.6 0.5 collective-permute-start.1
  93.2 1.3 fusion.11
  94.4 5.5 %collective-permute-start.4 = (f32[4,4,152]{1,2,0:T(8,128)S(1)}, f32[4,4,152]{1,2,0:T(8,128)S(1)}, u32[]{:S(2)}, u32[]{:S(2)}) collective-permute-start(f32[4,4,152]{1,2,0:T(8,128)S(1)} %get-tuple-element.11), channel_id=1, source_target_pairs={{0,9},{1,10},{2,11},{3,12},{4,13},{5,14},{6,15},{8,17},{9,18},{10,... | collective-permute-start | bytes 29192 | tf_op jit(solution)/shard_map/ppermute | solution.py:36
  99.9 2.2 collective-permute-start.6
  102.1 0.2 copy.56
  102.3 0.2 copy.60
  102.5 3.1 %collective-permute-start.7 = (f32[4,4,152]{1,2,0:T(8,128)S(1)}, f32[4,4,152]{1,2,0:T(8,128)S(1)}, u32[]{:S(2)}, u32[]{:S(2)}) collective-permute-start(f32[4,4,152]{1,2,0:T(8,128)S(1)} %get-tuple-element.10), channel_id=1, source_target_pairs={{1,8},{2,9},{3,10},{4,11},{5,12},{6,13},{7,14},{9,16},{10,17},{11,... | collective-permute-start | bytes 29192 | tf_op jit(solution)/shard_map/ppermute | solution.py:36
  105.6 4.0 %copy.52 = f32[64,4,152]{1,2,0:T(8,128)} copy(f32[64,4,152]{2,0,1:T(8,128)} %collective-permute-done) | data formatting | bytes 311296 | tf_op jit(solution)/shard_map/ppermute | solution.py:18
  109.6 5.1 %collective-permute-start.2 = (f32[4,152,128]{2,1,0:T(8,128)S(1)}, f32[4,152,128]{2,1,0:T(8,128)}, u32[]{:S(2)}, u32[]{:S(2)}) collective-permute-start(f32[4,152,128]{2,1,0:T(8,128)S(1)} %bitcast.54), channel_id=1, source_target_pairs={{0,1},{1,2},{2,3},{3,4},{4,5},{5,6},{6,7},{8,9},{9,10},{10,11},{11... | collective-permute-start | bytes 933896 | tf_op jit(solution)/shard_map/ppermute | solution.py:23
  114.7 4.1 %copy.54 = f32[64,4,152]{1,2,0:T(8,128)} copy(f32[64,4,152]{2,0,1:T(8,128)} %collective-permute-done.1) | data formatting | bytes 311296 | tf_op jit(solution)/shard_map/ppermute | solution.py:18
  118.8 1.9 collective-permute-start.5
  120.7 7.6 %pad_maximum_fusion.ew_ref = f32[64,152,128]{2,1,0:T(8,128)} fusion(f32[64,152,4]{2,1,0:T(8,128)} %bitcast.43, f32[64,152,4]{2,1,0:T(8,128)} %bitcast.42, f32[128]{0:T(128)S(1)} %pad.28.clone), kind=kLoop, calls=%fused_computation.2 | loop fusion | flops 2490368 | bytes 5292544 | tf_op jit(solution)/shard_map/concatenate | solution.py:92
  128.3 1.2 collective-permute-done.2
  129.5 2.2 %pad_maximum_fusion.2 = (f32[4,152,256]{2,1,0:T(8,128)}, f32[4,152,256]{2,1,0:T(8,128)}) fusion(f32[4,152,4]{2,1,0:T(8,128)S(1)} %bitcast.58, f32[4,152,4]{2,1,0:T(8,128)S(1)} %bitcast.57, f32[4,152,128]{2,1,0:T(8,128)S(1)} %collective-permute-done.5, f32[256]{0:T(256)S(1)} %pad.25.clone, f32[4,152,4]{2,1,0:T(8,128)S(1)} %bitcast.56, ...), kind=kLoop, calls=%fused_computation.12 | loop fusion | flops 933888 | bytes 1907712 | tf_op jit(solution)/shard_map/concatenate | solution.py:179
  131.8 0.7 broadcast_in_dim.44.lvl_ref
  132.5 82.9 %shard_map.73 = f32[64,150,128]{2,1,0:T(8,128)} custom-call(f32[64,152,128]{2,1,0:T(8,128)} %bitcast.44, f32[64,152,128]{2,1,0:T(8,128)} %pad_maximum_fusion.ew_ref, f32[4,152,256]{2,1,0:T(8,128)} %get-tuple-element.22.top_ref, f32[4,152,256]{2,1,0:T(8,128)} %get-tuple-element.21.bot_ref, f32[72,10,256]{2,1,0:T(8,128)} %maximum_maximum_fusion.s_ref, ...), custom_call_target="tpu_custom_call" | custom-call | flops 10444603392 | bytes 16121856 | tf_op jit(solution)/shard_map/pallas_call | solution.py:186
  215.4 5.6 %copy.65 = f32[150,64,128]{2,1,0:T(8,128)} copy(f32[150,64,128]{2,0,1:T(8,128)} %bitcast.45) | data formatting | bytes 9830400 | tf_op jit(solution)/shard_map/transpose | solution.py:242
  (58 shorter events, 2.0 us)
Async XLA Ops:
  8.5 10.2 %copy-start = (f32[9,64,128]{2,1,0:T(8,128)S(1)}, f32[9,64,128]{2,1,0:T(8,128)}, u32[]{:S(2)}) copy-start(f32[9,64,128]{2,1,0:T(8,128)} %param.11) | copy-start | bytes 884740
  8.5 10.4 %copy-start.2 = (s32[64,128]{1,0:T(8,128)S(1)}, s32[64,128]{1,0:T(8,128)}, u32[]{:S(2)}) copy-start(s32[64,128]{1,0:T(8,128)} %param.12) | copy-start | bytes 98308
  8.5 50.2 %all-to-all-start = ((f32[128,16,152]{2,1,0:T(8,128)}), f32[128,16,152]{2,1,0:T(8,128)S(1)}, u32[]{:S(2)}, u32[]{:S(2)}) async-start(f32[128,16,152]{2,1,0:T(8,128)} %bitcast.9), calls=%async_computation | async-start | bytes 4194304 | tf_op jit(solution)/shard_map/all_to_all | solution.py:233
  19.0 33.0 %copy-start.1 = (f32[150,150]{1,0:T(8,128)S(1)}, f32[150,150]{1,0:T(8,128)}, u32[]{:S(2)}) copy-start(f32[150,150]{1,0:T(8,128)} %param.13) | copy-start | bytes 270004
  19.2 26.1 %collective-permute-start.9 = (f32[160]{0:T(256)S(1)}, f32[160]{0:T(256)S(1)}, u32[]{:S(2)}, u32[]{:S(2)}) collective-permute-start(f32[160]{0:T(256)S(1)} %reshape.102), channel_id=1, source_target_pairs={{0,121},{1,122},{2,123},{3,124},{4,125},{5,126},{6,127},{8,1},{9,2... | collective-permute-start | bytes 1928 | tf_op jit(solution)/shard_map/ppermute | solution.py:36
  25.9 19.4 %collective-permute-start.10 = (f32[160]{0:T(256)S(1)}, f32[160]{0:T(256)S(1)}, u32[]{:S(2)}, u32[]{:S(2)}) collective-permute-start(f32[160]{0:T(256)S(1)} %reshape.104), channel_id=1, source_target_pairs={{0,9},{1,10},{2,11},{3,12},{4,13},{5,14},{6,15},{8,17},{9,18},{10,... | collective-permute-start | bytes 1928 | tf_op jit(solution)/shard_map/ppermute | solution.py:36
  28.0 21.8 %collective-permute-start.14 = (f32[160]{0:T(256)S(1)}, f32[160]{0:T(256)S(1)}, u32[]{:S(2)}, u32[]{:S(2)}) collective-permute-start(f32[160]{0:T(256)S(1)} %reshape.112), channel_id=1, source_target_pairs={{1,120},{2,121},{3,122},{4,123},{5,124},{6,125},{7,126},{9,0},{10,... | collective-permute-start | bytes 1928 | tf_op jit(solution)/shard_map/ppermute | solution.py:36
  33.8 19.3 %collective-permute-start.15 = (f32[160]{0:T(256)S(1)}, f32[160]{0:T(256)S(1)}, u32[]{:S(2)}, u32[]{:S(2)}) collective-permute-start(f32[160]{0:T(256)S(1)} %reshape.114), channel_id=1, source_target_pairs={{1,8},{2,9},{3,10},{4,11},{5,12},{6,13},{7,14},{9,16},{10,17},{11,... | collective-permute-start | bytes 1928 | tf_op jit(solution)/shard_map/ppermute | solution.py:36
  37.9 15.3 %collective-permute-start.11 = (f32[2560]{0:T(1024)S(1)}, f32[2560]{0:T(1024)S(1)}, u32[]{:S(2)}, u32[]{:S(2)}) collective-permute-start(f32[2560]{0:T(1024)S(1)} %reshape.106), channel_id=1, source_target_pairs={{0,120},{8,0},{16,8},{24,16},{32,24},{40,32},{48,40},{56,48},{64,5... | collective-permute-start | bytes 30728 | tf_op jit(solution)/shard_map/ppermute | solution.py:18
  45.3 8.1 %collective-permute-start.12 = (f32[2560]{0:T(1024)S(1)}, f32[2560]{0:T(1024)S(1)}, u32[]{:S(2)}, u32[]{:S(2)}) collective-permute-start(f32[2560]{0:T(1024)S(1)} %reshape.108), channel_id=1, source_target_pairs={{0,8},{8,16},{16,24},{24,32},{32,40},{40,48},{48,56},{56,64},{64,7... | collective-permute-start | bytes 30728 | tf_op jit(solution)/shard_map/ppermute | solution.py:18
  45.4 9.0 %collective-permute-start.8 = (f32[5120]{0:T(1024)S(1)}, f32[5120]{0:T(1024)S(1)}, u32[]{:S(2)}, u32[]{:S(2)}) collective-permute-start(f32[5120]{0:T(1024)S(1)} %reshape.100), channel_id=1, source_target_pairs={{0,1},{1,2},{2,3},{3,4},{4,5},{5,6},{6,7},{8,9},{9,10},{10,11},{11... | collective-permute-start | bytes 61448 | tf_op jit(solution)/shard_map/ppermute | solution.py:23
  49.8 6.6 %collective-permute-start.13 = (f32[5120]{0:T(1024)S(1)}, f32[5120]{0:T(1024)S(1)}, u32[]{:S(2)}, u32[]{:S(2)}) collective-permute-start(f32[5120]{0:T(1024)S(1)} %reshape.110), channel_id=1, source_target_pairs={{1,0},{2,1},{3,2},{4,3},{5,4},{6,5},{7,6},{9,8},{10,9},{11,10},{12... | collective-permute-start | bytes 61448 | tf_op jit(solution)/shard_map/ppermute | solution.py:23
  87.1 31.7 %collective-permute-start.3 = (f32[4,4,152]{1,2,0:T(8,128)S(1)}, f32[4,4,152]{1,2,0:T(8,128)S(1)}, u32[]{:S(2)}, u32[]{:S(2)}) collective-permute-start(f32[4,4,152]{1,2,0:T(8,128)S(1)} %get-tuple-element.12), channel_id=1, source_target_pairs={{0,121},{1,122},{2,123},{3,124},{4,125},{5,126},{6,127},{8,1},{9,2... | collective-permute-start | bytes 29192 | tf_op jit(solution)/shard_map/ppermute | solution.py:36
  91.9 10.6 %collective-permute-start = (f32[64,4,152]{2,0,1:T(8,128)}, f32[64,4,152]{2,0,1:T(8,128)}, u32[]{:S(2)}, u32[]{:S(2)}) collective-permute-start(f32[64,4,152]{2,0,1:T(8,128)} %copy.51), channel_id=1, source_target_pairs={{0,120},{8,0},{16,8},{24,16},{32,24},{40,32},{48,40},{56,48},{64,5... | collective-permute-start | bytes 466952 | tf_op jit(solution)/shard_map/ppermute | solution.py:18
  92.6 17.0 %collective-permute-start.1 = (f32[64,4,152]{2,0,1:T(8,128)}, f32[64,4,152]{2,0,1:T(8,128)}, u32[]{:S(2)}, u32[]{:S(2)}) collective-permute-start(f32[64,4,152]{2,0,1:T(8,128)} %copy.53), channel_id=1, source_target_pairs={{0,8},{8,16},{16,24},{24,32},{32,40},{40,48},{48,56},{56,64},{64,7... | collective-permute-start | bytes 466952 | tf_op jit(solution)/shard_map/ppermute | solution.py:18
  94.4 33.9 %collective-permute-start.4 = (f32[4,4,152]{1,2,0:T(8,128)S(1)}, f32[4,4,152]{1,2,0:T(8,128)S(1)}, u32[]{:S(2)}, u32[]{:S(2)}) collective-permute-start(f32[4,4,152]{1,2,0:T(8,128)S(1)} %get-tuple-element.11), channel_id=1, source_target_pairs={{0,9},{1,10},{2,11},{3,12},{4,13},{5,14},{6,15},{8,17},{9,18},{10,... | collective-permute-start | bytes 29192 | tf_op jit(solution)/shard_map/ppermute | solution.py:36
  99.9 28.4 %collective-permute-start.6 = (f32[4,4,152]{1,2,0:T(8,128)S(1)}, f32[4,4,152]{1,2,0:T(8,128)S(1)}, u32[]{:S(2)}, u32[]{:S(2)}) collective-permute-start(f32[4,4,152]{1,2,0:T(8,128)S(1)} %get-tuple-element.9), channel_id=1, source_target_pairs={{1,120},{2,121},{3,122},{4,123},{5,124},{6,125},{7,126},{9,0},{10,... | collective-permute-start | bytes 29192 | tf_op jit(solution)/shard_map/ppermute | solution.py:36
  102.5 25.8 %collective-permute-start.7 = (f32[4,4,152]{1,2,0:T(8,128)S(1)}, f32[4,4,152]{1,2,0:T(8,128)S(1)}, u32[]{:S(2)}, u32[]{:S(2)}) collective-permute-start(f32[4,4,152]{1,2,0:T(8,128)S(1)} %get-tuple-element.10), channel_id=1, source_target_pairs={{1,8},{2,9},{3,10},{4,11},{5,12},{6,13},{7,14},{9,16},{10,17},{11,... | collective-permute-start | bytes 29192 | tf_op jit(solution)/shard_map/ppermute | solution.py:36
  109.6 19.9 %collective-permute-start.2 = (f32[4,152,128]{2,1,0:T(8,128)S(1)}, f32[4,152,128]{2,1,0:T(8,128)}, u32[]{:S(2)}, u32[]{:S(2)}) collective-permute-start(f32[4,152,128]{2,1,0:T(8,128)S(1)} %bitcast.54), channel_id=1, source_target_pairs={{0,1},{1,2},{2,3},{3,4},{4,5},{5,6},{6,7},{8,9},{9,10},{10,11},{11... | collective-permute-start | bytes 933896 | tf_op jit(solution)/shard_map/ppermute | solution.py:23
  118.8 10.7 %collective-permute-start.5 = (f32[4,152,128]{2,1,0:T(8,128)S(1)}, f32[4,152,128]{2,1,0:T(8,128)S(1)}, u32[]{:S(2)}, u32[]{:S(2)}) collective-permute-start(f32[4,152,128]{2,1,0:T(8,128)S(1)} %bitcast.53), channel_id=1, source_target_pairs={{1,0},{2,1},{3,2},{4,3},{5,4},{6,5},{7,6},{9,8},{10,9},{11,10},{12... | collective-permute-start | bytes 933896 | tf_op jit(solution)/shard_map/ppermute | solution.py:23

commit v4 on v3

--- a/solution.py
+++ b/solution.py
@@ -76,8 +76,8 @@
         return jnp.transpose(a, (0, 2, 1))
 
     return {
-        "west": t(shift_lon(f[:, cols - r :, :], 1)),
-        "east": t(shift_lon(f[:, :r, :], -1)),
+        "west": shift_lon(f[:, cols - r :, :], 1),
+        "east": shift_lon(f[:, :r, :], -1),
         "south": shift_lat(v_bot, 1),
         "north": shift_lat(v_top, -1),
         "sw": t(shift_both(f[rows - r :, cols - r :, :], 1, 1)),
@@ -112,15 +112,18 @@
 ):
     full = p_ref.shape[0]
     rows = v_ref.shape[0]
-    cols = v_ref.shape[2]
+    cols = v_ref.shape[1]
     chans = p_ref.shape[1]
     out_ch = out_ref.shape[1]
     p_ref[:RADIUS] = top_ref[...]
     p_ref[full - RADIUS :] = bot_ref[...]
 
     def fill(y, carry):
-        p_ref[y + RADIUS, :, :cols] = v_ref[y]
-        p_ref[y + RADIUS, :, cols:] = ew_ref[y]
+        p_ref[y + RADIUS, :, :cols] = jnp.transpose(v_ref[y])
+        p_ref[y + RADIUS, :, cols:] = jnp.zeros((chans, LANES - cols), jnp.float32)
+        sides = jnp.transpose(ew_ref[y])
+        p_ref[y + RADIUS, :, cols : cols + RADIUS] = sides[:, :RADIUS]
+        p_ref[y + RADIUS, :, LANES - RADIUS :] = sides[:, RADIUS:]
         return carry
 
     lax.fori_loop(0, rows, fill, 0)
@@ -169,12 +172,11 @@
         lax.fori_loop(p + 1, full - 1 - p, row, 0, unroll=2)
 
 
-def run_passes(field_pm, halos, stat, balance, chans):
-    field = jnp.transpose(field_pm, (0, 2, 1))
-    rows, cpad, cols = field.shape
+def run_passes(field, halos, stat, balance, chans):
+    rows, cols, cpad = field.shape
     full = rows + 2 * RADIUS
     gap = LANES - cols - 2 * RADIUS
-    ew = side_lanes(halos["east"], halos["west"], gap)
+    ew = jnp.concatenate([halos["east"], halos["west"]], axis=1)
     top = jnp.concatenate([halos["south"], side_lanes(halos["se"], halos["sw"], gap)], axis=2)
     bot = jnp.concatenate([halos["north"], side_lanes(halos["ne"], halos["nw"], gap)], axis=2)
     lvl = jnp.broadcast_to(

time: 223 us -> 221 us (level)
  local copies, waits for them, and re-layouts: 38.9 us -> 27.3 us
  Pallas kernels: 82.9 us -> 93.1 us
  other arithmetic: 33.3 us -> 23.9 us
  waiting for transfers between devices: 3.27 us -> 8.4 us
  starting transfers between devices: 62.3 us -> 64.7 us
    pallas_call x1, Pallas kernels: 82.9 us -> 93.1 us  [run_passes(): pl.pallas_call(passes_kernel, out_shape=jax.ShapeDtypeStruct((rows, chans...]
    ppermute x8, waiting for transfers between devices: 0.02 us -> 8.37 us  [shift_both(): return lax.ppermute(block, ('lon', 'lat'), pairs)]
    reshape x1 -> x0, local copies, waits for them, and re-layouts: 8.26 us -> none  [local(): field = field.reshape(rows_y, cols_x, CPAD)]
    ppermute x2 -> x0, local copies, waits for them, and re-layouts: 8.06 us -> none  [shift_lon(): lax.ppermute(block, 'lon', [(i, (i + step) % count) for i in range(count)])]
    concatenate x1, other arithmetic: 7.58 us -> 1.95 us  [run_passes(): ew = jnp.concatenate([halos['east'], halos['west']], axis=1)]
    ppermute x4, starting transfers between devices: 7.78 us -> 12.4 us  [shift_lon(): lax.ppermute(block, 'lon', [(i, (i + step) % count) for i in range(count)])]
    reshape x8, local copies, waits for them, and re-layouts: 1.52 us -> 5.85 us  [exchange(): got[i][name] = flat[offset:offset + p.size].reshape(p.shape)]
    ppermute x4, waiting for transfers between devices: 3.24 us -> 0.01 us  [shift_lat(): lax.ppermute(block, 'lat', [(i, i + step) for i in range(count) if 0 <= i...]
  transfers between devices with their start and end apart: 17 -> 17, of which waited for: 2 -> 3; matrix products, arithmetic and copies ran while one was open for 12% -> 7% of each run, Pallas kernels for 0% -> 0%
where the time goes in v4:
time: 221 us; the launch traced here: 218 us
  Pallas kernels  93.1 us (42%)
  starting transfers between devices  64.7 us (29%)
  local copies, waits for them, and re-layouts  27.3 us (12%)
  other arithmetic  23.9 us (11%)
  waiting for transfers between devices  8.4 us (4%)
    pallas_call x1, Pallas kernels, run_passes(): pl.pallas_call(passes_kernel, out_shape=jax.ShapeDtypeStruct((rows, chans...  93.1 us
    ppermute x8, starting transfers between devices, shift_both(): return lax.ppermute(block, ('lon', 'lat'), pairs)  29.4 us
    scatter-add x1, other arithmetic, local(): field = jnp.zeros((rows_y * cols_x, CPAD), jnp.float32).at[where].add(got)  16.1 us
    ppermute x4, starting transfers between devices, shift_lat(): lax.ppermute(block, 'lat', [(i, i + step) for i in range(count) if 0 <= i...  12.8 us
    ppermute x4, starting transfers between devices, shift_lon(): lax.ppermute(block, 'lon', [(i, (i + step) % count) for i in range(count)])  12.4 us
    all_to_all x1, starting transfers between devices, local(): lax.all_to_all(send.reshape(devices, capacity, CPAD), ('lon', 'lat'), 0,...  10.2 us
    ppermute x8, waiting for transfers between devices, shift_both(): return lax.ppermute(block, ('lon', 'lat'), pairs)  8.37 us
    reshape x8, local copies, waits for them, and re-layouts, exchange(): got[i][name] = flat[offset:offset + p.size].reshape(p.shape)  5.85 us
  transfers between devices with their start and end apart: 17, of which 3 were waited for; matrix products, arithmetic and copies ran while one was open for 7% of the time, Pallas kernels for 0%

profile of v4, /device:TPU:34, one launch (start us, length us, event | category | flops | bytes accessed | tf_op | source)
XLA Modules:
  0.0 217.9 jit_solution(15150928251175551765)
XLA Ops:
  0.0 0.7 convert_element_type.28
  0.8 0.8 copy.30
  1.5 0.2 fusion.7
  1.9 0.2 fusion.6
  2.4 0.2 copy.32
  2.6 3.6 %scatter_custom_fusion = f32[2048,152]{1,0:T(8,128)} fusion(s32[512]{0:T(512)S(1)} %bitcast.60, f32[512,152]{1,0:T(8,128)S(1)} %copy.32, f32[]{:T(128)} %constant.13.clone.1), kind=kCustom, calls=%fused_computation.8 | custom fusion | bytes 1245188 | tf_op jit(solution)/shard_map/scatter | solution.py:234
  6.2 10.2 %all-to-all-start = ((f32[128,16,152]{2,1,0:T(8,128)}), f32[128,16,152]{2,1,0:T(8,128)S(1)}, u32[]{:S(2)}, u32[]{:S(2)}) async-start(f32[128,16,152]{2,1,0:T(8,128)} %bitcast.9), calls=%async_computation | async-start | bytes 4194304 | tf_op jit(solution)/shard_map/all_to_all | solution.py:235
  16.8 2.3 %collective-permute-start.13 = (f32[5120]{0:T(1024)S(1)}, f32[5120]{0:T(1024)S(1)}, u32[]{:S(2)}, u32[]{:S(2)}) collective-permute-start(f32[5120]{0:T(1024)S(1)} %reshape.110), channel_id=1, source_target_pairs={{1,0},{2,1},{3,2},{4,3},{5,4},{6,5},{7,6},{9,8},{10,9},{11,10},{12... | collective-permute-start | bytes 61448 | tf_op jit(solution)/shard_map/ppermute | solution.py:23
  19.1 4.4 %collective-permute-start.8 = (f32[5120]{0:T(1024)S(1)}, f32[5120]{0:T(1024)S(1)}, u32[]{:S(2)}, u32[]{:S(2)}) collective-permute-start(f32[5120]{0:T(1024)S(1)} %reshape.100), channel_id=1, source_target_pairs={{0,1},{1,2},{2,3},{3,4},{4,5},{5,6},{6,7},{8,9},{9,10},{10,11},{11... | collective-permute-start | bytes 61448 | tf_op jit(solution)/shard_map/ppermute | solution.py:23
  23.8 4.2 %collective-permute-start.14 = (f32[160]{0:T(256)S(1)}, f32[160]{0:T(256)S(1)}, u32[]{:S(2)}, u32[]{:S(2)}) collective-permute-start(f32[160]{0:T(256)S(1)} %reshape.112), channel_id=1, source_target_pairs={{1,120},{2,121},{3,122},{4,123},{5,124},{6,125},{7,126},{9,0},{10,... | collective-permute-start | bytes 1928 | tf_op jit(solution)/shard_map/ppermute | solution.py:36
  28.1 1.9 collective-permute-start.15
  30.1 6.8 %collective-permute-start.9 = (f32[160]{0:T(256)S(1)}, f32[160]{0:T(256)S(1)}, u32[]{:S(2)}, u32[]{:S(2)}) collective-permute-start(f32[160]{0:T(256)S(1)} %reshape.102), channel_id=1, source_target_pairs={{0,121},{1,122},{2,123},{3,124},{4,125},{5,126},{6,127},{8,1},{9,2... | collective-permute-start | bytes 1928 | tf_op jit(solution)/shard_map/ppermute | solution.py:36
  36.9 0.9 fusion.16
  37.9 0.6 reshape.104
  38.5 1.2 reshape.106
  39.9 1.9 collective-permute-start.10
  41.8 1.4 collective-permute-done.15
  43.2 0.9 collective-permute-start.12
  44.1 5.9 %collective-permute-start.11 = (f32[2560]{0:T(1024)S(1)}, f32[2560]{0:T(1024)S(1)}, u32[]{:S(2)}, u32[]{:S(2)}) collective-permute-start(f32[2560]{0:T(1024)S(1)} %reshape.106), channel_id=1, source_target_pairs={{0,120},{8,0},{16,8},{24,16},{32,24},{40,32},{48,40},{56,48},{64,5... | collective-permute-start | bytes 30728 | tf_op jit(solution)/shard_map/ppermute | solution.py:18
  50.3 0.7 pad.4.bal_ref
  51.0 1.3 reshape.103
  52.3 0.7 reshape.115
  53.0 0.7 reshape.113
  53.7 0.7 reshape.105
  54.6 1.0 reshape.109
  55.7 0.6 reshape.111
  56.3 0.6 reshape.101
  56.9 0.6 fusion.2
  57.5 16.1 %scatter_custom_fusion.1 = f32[8192,152]{1,0:T(8,128)} fusion(s32[2048]{0:T(1024)S(1)} %fusion.2, f32[2048,152]{1,0:T(8,128)S(1)} %bitcast.43, f32[]{:T(128)} %constant.13.clone.1), kind=kCustom, calls=%fused_computation.2 | custom fusion | flops 311296 | bytes 4980740 | tf_op jit(solution)/shard_map/scatter-add | solution.py:239
  73.7 1.4 fusion.12
  75.1 2.1 fusion.13
  77.2 1.3 fusion.11
  78.7 1.9 collective-permute-start.7
  80.6 5.6 %collective-permute-start = (f32[64,4,152]{2,1,0:T(4,128)}, f32[64,4,152]{2,1,0:T(4,128)}, u32[]{:S(2)}, u32[]{:S(2)}) collective-permute-start(f32[64,4,152]{2,1,0:T(4,128)} %get-tuple-element.11), channel_id=1, source_target_pairs={{0,120},{8,0},{16,8},{24,16},{32,24},{40,32},{48,40},{56,48},{64,5... | collective-permute-start | bytes 466952 | tf_op jit(solution)/shard_map/ppermute | solution.py:18
  86.4 0.2 copy.37
  86.6 3.4 %collective-permute-start.2 = (f32[4,152,128]{2,1,0:T(8,128)S(1)}, f32[4,152,128]{2,1,0:T(8,128)S(1)}, u32[]{:S(2)}, u32[]{:S(2)}) collective-permute-start(f32[4,152,128]{2,1,0:T(8,128)S(1)} %bitcast.50), channel_id=1, source_target_pairs={{0,1},{1,2},{2,3},{3,4},{4,5},{5,6},{6,7},{8,9},{9,10},{10,11},{11... | collective-permute-start | bytes 933896 | tf_op jit(solution)/shard_map/ppermute | solution.py:23
  90.0 2.6 %collective-permute-start.5 = (f32[4,152,128]{2,1,0:T(8,128)S(1)}, f32[4,152,128]{2,1,0:T(8,128)}, u32[]{:S(2)}, u32[]{:S(2)}) collective-permute-start(f32[4,152,128]{2,1,0:T(8,128)S(1)} %bitcast.49), channel_id=1, source_target_pairs={{1,0},{2,1},{3,2},{4,3},{5,4},{6,5},{7,6},{9,8},{10,9},{11,10},{12... | collective-permute-start | bytes 933896 | tf_op jit(solution)/shard_map/ppermute | solution.py:23
  92.7 1.3 maximum_maximum_fusion.s_ref
  94.5 1.9 collective-permute-done.7
  96.5 4.9 %collective-permute-start.3 = (f32[4,4,152]{1,2,0:T(8,128)S(1)}, f32[4,4,152]{1,2,0:T(8,128)S(1)}, u32[]{:S(2)}, u32[]{:S(2)}) collective-permute-start(f32[4,4,152]{1,2,0:T(8,128)S(1)} %copy.54), channel_id=1, source_target_pairs={{0,121},{1,122},{2,123},{3,124},{4,125},{5,126},{6,127},{8,1},{9,2... | collective-permute-start | bytes 29192 | tf_op jit(solution)/shard_map/ppermute | solution.py:36
  101.4 1.9 collective-permute-start.4
  103.3 5.8 %collective-permute-start.6 = (f32[4,4,152]{1,2,0:T(8,128)S(1)}, f32[4,4,152]{1,2,0:T(8,128)S(1)}, u32[]{:S(2)}, u32[]{:S(2)}) collective-permute-start(f32[4,4,152]{1,2,0:T(8,128)S(1)} %copy.56), channel_id=1, source_target_pairs={{1,120},{2,121},{3,122},{4,123},{5,124},{6,125},{7,126},{9,0},{10,... | collective-permute-start | bytes 29192 | tf_op jit(solution)/shard_map/ppermute | solution.py:36
  109.1 1.9 pad_maximum_fusion.2.ew_ref
  111.1 5.0 %collective-permute-done.3 = f32[4,4,152]{1,2,0:T(8,128)S(1)} collective-permute-done((f32[4,4,152]{1,2,0:T(8,128)S(1)}, f32[4,4,152]{1,2,0:T(8,128)S(1)}, u32[]{:S(2)}, u32[]{:S(2)}) %collective-permute-start.3) | collective-permute-done | bytes 9760 | tf_op jit(solution)/shard_map/ppermute | solution.py:36
  116.1 2.4 %pad_maximum_fusion.1 = (f32[4,152,256]{2,1,0:T(8,128)}, f32[4,152,256]{2,1,0:T(8,128)}) fusion(f32[4,152,4]{2,1,0:T(8,128)} %bitcast.19, f32[4,152,4]{2,1,0:T(8,128)S(1)} %bitcast.53, f32[4,152,128]{2,1,0:T(8,128)} %collective-permute-done.5, f32[256]{0:T(256)S(1)} %pad.25.clone, f32[4,152,4]{2,1,0:T(8,128)S(1)} %bitcast.52, f32[4,152,4]{2,1,0:T(8,128)S(1)} %bitcast.51, ...), kind=kLoop, calls=%fused_computation.11 | loop fusion | flops 933888 | bytes 1907712 | tf_op jit(solution)/shard_map/concatenate | solution.py:181
  118.5 0.8 broadcast_in_dim.40.lvl_ref
  119.2 93.1 %shard_map.73 = f32[64,150,128]{2,1,0:T(8,128)} custom-call(f32[64,128,152]{2,1,0:T(8,128)} %bitcast.40, f32[64,8,152]{2,1,0:T(8,128)} %pad_maximum_fusion.2.ew_ref, f32[4,152,256]{2,1,0:T(8,128)} %get-tuple-element.22.top_ref, f32[4,152,256]{2,1,0:T(8,128)} %get-tuple-element.21.bot_ref, f32[72,10,256]{2,1,0:T(8,128)} %maximum_maximum_fusion.s_ref, ...), custom_call_target="tpu_custom_call" | custom-call | flops 10444603392 | bytes 16121856 | tf_op jit(solution)/shard_map/pallas_call | solution.py:188
  212.3 5.6 %copy.47 = f32[150,64,128]{2,1,0:T(8,128)} copy(f32[150,64,128]{2,0,1:T(8,128)} %bitcast.41) | data formatting | bytes 9830400 | tf_op jit(solution)/shard_map/transpose | solution.py:244
  (80 shorter events, 2.6 us)
Async XLA Ops:
  0.0 1.9 copy-start.12
  0.0 2.2 %copy-start.13 = (s32[512]{0:T(512)S(1)}, s32[512]{0:T(512)}, u32[]{:S(2)}) copy-start(s32[512]{0:T(512)} %param.10) | copy-start | bytes 6148
  0.0 2.2 %copy-start.1 = (f32[150,512]{1,0:T(8,128)S(1)}, f32[150,512]{1,0:T(8,128)}, u32[]{:S(2)}) copy-start(f32[150,512]{1,0:T(8,128)} %param.7) | copy-start | bytes 921604
  6.2 10.2 %copy-start.11 = (s32[64,128]{1,0:T(8,128)S(1)}, s32[64,128]{1,0:T(8,128)}, u32[]{:S(2)}) copy-start(s32[64,128]{1,0:T(8,128)} %param.12) | copy-start | bytes 98308
  6.2 10.2 %copy-start.2 = (f32[9,64,128]{2,1,0:T(8,128)S(1)}, f32[9,64,128]{2,1,0:T(8,128)}, u32[]{:S(2)}) copy-start(f32[9,64,128]{2,1,0:T(8,128)} %param.11) | copy-start | bytes 884740
  6.2 50.6 %all-to-all-start = ((f32[128,16,152]{2,1,0:T(8,128)}), f32[128,16,152]{2,1,0:T(8,128)S(1)}, u32[]{:S(2)}, u32[]{:S(2)}) async-start(f32[128,16,152]{2,1,0:T(8,128)} %bitcast.9), calls=%async_computation | async-start | bytes 4194304 | tf_op jit(solution)/shard_map/all_to_all | solution.py:235
  16.8 38.9 %collective-permute-start.13 = (f32[5120]{0:T(1024)S(1)}, f32[5120]{0:T(1024)S(1)}, u32[]{:S(2)}, u32[]{:S(2)}) collective-permute-start(f32[5120]{0:T(1024)S(1)} %reshape.110), channel_id=1, source_target_pairs={{1,0},{2,1},{3,2},{4,3},{5,4},{6,5},{7,6},{9,8},{10,9},{11,10},{12... | collective-permute-start | bytes 61448 | tf_op jit(solution)/shard_map/ppermute | solution.py:23
  19.1 37.1 %collective-permute-start.8 = (f32[5120]{0:T(1024)S(1)}, f32[5120]{0:T(1024)S(1)}, u32[]{:S(2)}, u32[]{:S(2)}) collective-permute-start(f32[5120]{0:T(1024)S(1)} %reshape.100), channel_id=1, source_target_pairs={{0,1},{1,2},{2,3},{3,4},{4,5},{5,6},{6,7},{8,9},{9,10},{10,11},{11... | collective-permute-start | bytes 61448 | tf_op jit(solution)/shard_map/ppermute | solution.py:23
  23.8 16.1 %collective-permute-start.14 = (f32[160]{0:T(256)S(1)}, f32[160]{0:T(256)S(1)}, u32[]{:S(2)}, u32[]{:S(2)}) collective-permute-start(f32[160]{0:T(256)S(1)} %reshape.112), channel_id=1, source_target_pairs={{1,120},{2,121},{3,122},{4,123},{5,124},{6,125},{7,126},{9,0},{10,... | collective-permute-start | bytes 1928 | tf_op jit(solution)/shard_map/ppermute | solution.py:36
  28.1 15.1 %collective-permute-start.15 = (f32[160]{0:T(256)S(1)}, f32[160]{0:T(256)S(1)}, u32[]{:S(2)}, u32[]{:S(2)}) collective-permute-start(f32[160]{0:T(256)S(1)} %reshape.114), channel_id=1, source_target_pairs={{1,8},{2,9},{3,10},{4,11},{5,12},{6,13},{7,14},{9,16},{10,17},{11,... | collective-permute-start | bytes 1928 | tf_op jit(solution)/shard_map/ppermute | solution.py:36
  30.1 20.1 %copy-start.3 = (f32[150,150]{1,0:T(8,128)S(1)}, f32[150,150]{1,0:T(8,128)}, u32[]{:S(2)}) copy-start(f32[150,150]{1,0:T(8,128)} %param.13) | copy-start | bytes 270004
  30.1 14.0 %collective-permute-start.9 = (f32[160]{0:T(256)S(1)}, f32[160]{0:T(256)S(1)}, u32[]{:S(2)}, u32[]{:S(2)}) collective-permute-start(f32[160]{0:T(256)S(1)} %reshape.102), channel_id=1, source_target_pairs={{0,121},{1,122},{2,123},{3,124},{4,125},{5,126},{6,127},{8,1},{9,2... | collective-permute-start | bytes 1928 | tf_op jit(solution)/shard_map/ppermute | solution.py:36
  39.9 13.9 %collective-permute-start.10 = (f32[160]{0:T(256)}, f32[160]{0:T(256)S(1)}, u32[]{:S(2)}, u32[]{:S(2)}) collective-permute-start(f32[160]{0:T(256)} %reshape.104), channel_id=1, source_target_pairs={{0,9},{1,10},{2,11},{3,12},{4,13},{5,14},{6,15},{8,17},{9,18},{10,... | collective-permute-start | bytes 1928 | tf_op jit(solution)/shard_map/ppermute | solution.py:36
  43.2 11.4 %collective-permute-start.12 = (f32[2560]{0:T(1024)S(1)}, f32[2560]{0:T(1024)S(1)}, u32[]{:S(2)}, u32[]{:S(2)}) collective-permute-start(f32[2560]{0:T(1024)S(1)} %reshape.108), channel_id=1, source_target_pairs={{0,8},{8,16},{16,24},{24,32},{32,40},{40,48},{48,56},{56,64},{64,7... | collective-permute-start | bytes 30728 | tf_op jit(solution)/shard_map/ppermute | solution.py:18
  44.1 6.0 %copy-start.14 = (f32[160]{0:T(256)}, f32[160]{0:T(256)S(1)}, u32[]{:S(2)}) copy-start(f32[160]{0:T(256)S(1)} %collective-permute-done.9) | copy-start | bytes 1924
  44.1 10.3 %collective-permute-start.11 = (f32[2560]{0:T(1024)S(1)}, f32[2560]{0:T(1024)S(1)}, u32[]{:S(2)}, u32[]{:S(2)}) collective-permute-start(f32[2560]{0:T(1024)S(1)} %reshape.106), channel_id=1, source_target_pairs={{0,120},{8,0},{16,8},{24,16},{32,24},{40,32},{48,40},{56,48},{64,5... | collective-permute-start | bytes 30728 | tf_op jit(solution)/shard_map/ppermute | solution.py:18
  78.4 14.2 %copy-start = (f32[64,10,4]{2,1,0:T(8,128)S(1)}, f32[64,10,4]{2,1,0:T(8,128)}, u32[]{:S(2)}) copy-start(f32[64,10,4]{2,1,0:T(8,128)} %reshape.109) | copy-start | bytes 30724
  78.4 14.2 %copy-start.4 = (f32[4,10,4]{2,1,0:T(8,128)S(1)}, f32[4,10,4]{2,1,0:T(8,128)}, u32[]{:S(2)}) copy-start(f32[4,10,4]{2,1,0:T(8,128)} %reshape.103) | copy-start | bytes 1924
  78.4 14.2 %copy-start.5 = (f32[4,10,4]{2,1,0:T(8,128)S(1)}, f32[4,10,4]{2,1,0:T(8,128)}, u32[]{:S(2)}) copy-start(f32[4,10,4]{2,1,0:T(8,128)} %reshape.115) | copy-start | bytes 1924
  78.5 14.2 %copy-start.6 = (f32[4,10,4]{2,1,0:T(8,128)S(1)}, f32[4,10,4]{2,1,0:T(8,128)}, u32[]{:S(2)}) copy-start(f32[4,10,4]{2,1,0:T(8,128)} %reshape.113) | copy-start | bytes 1924
  78.5 14.2 %copy-start.7 = (f32[4,10,4]{2,1,0:T(8,128)S(1)}, f32[4,10,4]{2,1,0:T(8,128)}, u32[]{:S(2)}) copy-start(f32[4,10,4]{2,1,0:T(8,128)} %reshape.105) | copy-start | bytes 1924
  78.5 14.2 %copy-start.8 = (f32[4,10,128]{2,1,0:T(8,128)S(1)}, f32[4,10,128]{2,1,0:T(8,128)}, u32[]{:S(2)}) copy-start(f32[4,10,128]{2,1,0:T(8,128)} %reshape.111) | copy-start | bytes 61444
  78.5 14.2 %copy-start.9 = (f32[4,10,128]{2,1,0:T(8,128)S(1)}, f32[4,10,128]{2,1,0:T(8,128)}, u32[]{:S(2)}) copy-start(f32[4,10,128]{2,1,0:T(8,128)} %reshape.101) | copy-start | bytes 61444
  78.7 17.8 %collective-permute-start.7 = (f32[4,4,152]{1,2,0:T(8,128)S(1)}, f32[4,4,152]{1,2,0:T(8,128)}, u32[]{:S(2)}, u32[]{:S(2)}) collective-permute-start(f32[4,4,152]{1,2,0:T(8,128)S(1)} %copy.57), channel_id=1, source_target_pairs={{1,8},{2,9},{3,10},{4,11},{5,12},{6,13},{7,14},{9,16},{10,17},{11,... | collective-permute-start | bytes 29192 | tf_op jit(solution)/shard_map/ppermute | solution.py:36
  80.6 20.8 %collective-permute-start = (f32[64,4,152]{2,1,0:T(4,128)}, f32[64,4,152]{2,1,0:T(4,128)}, u32[]{:S(2)}, u32[]{:S(2)}) collective-permute-start(f32[64,4,152]{2,1,0:T(4,128)} %get-tuple-element.11), channel_id=1, source_target_pairs={{0,120},{8,0},{16,8},{24,16},{32,24},{40,32},{48,40},{56,48},{64,5... | collective-permute-start | bytes 466952 | tf_op jit(solution)/shard_map/ppermute | solution.py:18
  86.2 17.2 %collective-permute-start.1 = (f32[64,4,152]{2,1,0:T(4,128)}, f32[64,4,152]{2,1,0:T(4,128)}, u32[]{:S(2)}, u32[]{:S(2)}) collective-permute-start(f32[64,4,152]{2,1,0:T(4,128)} %get-tuple-element.12), channel_id=1, source_target_pairs={{0,8},{8,16},{16,24},{24,32},{32,40},{40,48},{48,56},{56,64},{64,7... | collective-permute-start | bytes 466952 | tf_op jit(solution)/shard_map/ppermute | solution.py:18
  86.6 29.5 %collective-permute-start.2 = (f32[4,152,128]{2,1,0:T(8,128)S(1)}, f32[4,152,128]{2,1,0:T(8,128)S(1)}, u32[]{:S(2)}, u32[]{:S(2)}) collective-permute-start(f32[4,152,128]{2,1,0:T(8,128)S(1)} %bitcast.50), channel_id=1, source_target_pairs={{0,1},{1,2},{2,3},{3,4},{4,5},{5,6},{6,7},{8,9},{9,10},{10,11},{11... | collective-permute-start | bytes 933896 | tf_op jit(solution)/shard_map/ppermute | solution.py:23
  90.0 26.1 %collective-permute-start.5 = (f32[4,152,128]{2,1,0:T(8,128)S(1)}, f32[4,152,128]{2,1,0:T(8,128)}, u32[]{:S(2)}, u32[]{:S(2)}) collective-permute-start(f32[4,152,128]{2,1,0:T(8,128)S(1)} %bitcast.49), channel_id=1, source_target_pairs={{1,0},{2,1},{3,2},{4,3},{5,4},{6,5},{7,6},{9,8},{10,9},{11,10},{12... | collective-permute-start | bytes 933896 | tf_op jit(solution)/shard_map/ppermute | solution.py:23
  92.7 1.5 copy-start.10
  96.5 19.6 %collective-permute-start.3 = (f32[4,4,152]{1,2,0:T(8,128)S(1)}, f32[4,4,152]{1,2,0:T(8,128)S(1)}, u32[]{:S(2)}, u32[]{:S(2)}) collective-permute-start(f32[4,4,152]{1,2,0:T(8,128)S(1)} %copy.54), channel_id=1, source_target_pairs={{0,121},{1,122},{2,123},{3,124},{4,125},{5,126},{6,127},{8,1},{9,2... | collective-permute-start | bytes 29192 | tf_op jit(solution)/shard_map/ppermute | solution.py:36
  101.4 14.7 %collective-permute-start.4 = (f32[4,4,152]{1,2,0:T(8,128)S(1)}, f32[4,4,152]{1,2,0:T(8,128)S(1)}, u32[]{:S(2)}, u32[]{:S(2)}) collective-permute-start(f32[4,4,152]{1,2,0:T(8,128)S(1)} %copy.55), channel_id=1, source_target_pairs={{0,9},{1,10},{2,11},{3,12},{4,13},{5,14},{6,15},{8,17},{9,18},{10,... | collective-permute-start | bytes 29192 | tf_op jit(solution)/shard_map/ppermute | solution.py:36
  103.3 12.7 %collective-permute-start.6 = (f32[4,4,152]{1,2,0:T(8,128)S(1)}, f32[4,4,152]{1,2,0:T(8,128)S(1)}, u32[]{:S(2)}, u32[]{:S(2)}) collective-permute-start(f32[4,4,152]{1,2,0:T(8,128)S(1)} %copy.56), channel_id=1, source_target_pairs={{1,120},{2,121},{3,122},{4,123},{5,124},{6,125},{7,126},{9,0},{10,... | collective-permute-start | bytes 29192 | tf_op jit(solution)/shard_map/ppermute | solution.py:36
